TPU v7x, 32 devices: a whole 2x2x4 slice. The times are simulated.
32 devices in a mesh: pole: 2 (over x), row: 8 (over z, y), col: 2 (over core).
Axes of the slice: x: 2, y: 2, z: 4, core: 2. Of those that a mesh axis runs over, the one named last changes fastest.
Arguments:
- anc_inverse: bfloat16 [2048, 1024], P(('pole', 'row')), parts along dimension 0, as said below
- parent_pivinv: float32 [2048, 1024], P(('pole', 'row')), parts along dimension 0, as said below
- parent_lower: bfloat16 [2048, 1024], P(('pole', 'row')), parts along dimension 0, may hold values from -0.1875 to 0.1875
- parent_mask: int32 [4], replicated, may hold values 0 or 1
- leaf_lower_par: bfloat16 [2048, 1024], P(('pole', 'row')), parts along dimension 0, may hold values from -0.125 to 0.125
- leaf_lower_anc: bfloat16 [2048, 1024], P(('pole', 'row')), parts along dimension 0, may hold values from -0.125 to 0.125
- leaf_mask: int32 [8], replicated, may hold values 0 or 1
- leaf_pivots: float32 [2048], P(('pole', 'col')), parts along dimension 0, may hold values from 0.5 to 2
Outputs:
- parent_block: float32 [2048, 1024], P(('pole', 'row')), parts along dimension 0
- parent_offdiag: bfloat16 [2048, 1024], P(('pole', 'row'), 'col'), parts along dimension 0
- leaf_par_block: bfloat16 [2048, 1024], P(('pole', 'row'), 'col'), parts along dimension 0
- leaf_anc_block: bfloat16 [2048, 1024], P(('pole', 'row'), 'col'), parts along dimension 0
- density: float32 [2048], P(('pole', 'col')), parts along dimension 0
There are 2 independent parts, one for each index of `pole`. A program takes and returns all parts, laid end to end along the dimension named above; an argument that names none is the same for every part. Nothing has to cross between parts.
Inputs may be any that keep to these rules, and one draw needn't show every extreme that they name: `anc_inverse`: symmetric. `parent_pivinv`: symmetric. `parent_mask`: 1 marks a structurally nonzero block of 256 rows. `leaf_mask`: 1 marks a structurally nonzero block of 256 rows.
All inputs are finite; a program needn't handle non-finite values.
Results may differ from a plain program's by a relative error of at most 0.0095.
Values may be sent and summed in bfloat16 or wider, within the bound.
No kernel may reach another device: no remote copies, remote signals or barrier semaphores. Data moves between devices by JAX's collectives and lax.ppermute only.
A program may use at most 64 MiB of HBM per device.

v0:
```python
import jax
import jax.numpy as jnp
from jax import lax
from jax.sharding import PartitionSpec as P

BLOCK = 256
ORDER = 1024


def local(
    anc_inverse,
    parent_pivinv,
    parent_lower,
    parent_mask,
    leaf_lower_par,
    leaf_lower_anc,
    leaf_mask,
    leaf_pivots,
):
    row_index = lax.axis_index("row")
    row_devices = lax.axis_size("row")
    col_index = lax.axis_index("col")
    anc_rows = anc_inverse.shape[0]
    order_rows = parent_pivinv.shape[0]
    col_width = leaf_pivots.shape[0]
    parent_gate = lax.dynamic_slice_in_dim(
        jnp.repeat(parent_mask, BLOCK), row_index * anc_rows, anc_rows
    )
    lower_one = parent_lower * parent_gate[:, None].astype(jnp.bfloat16)
    lower_half = lax.dynamic_slice_in_dim(lower_one, col_index * col_width, col_width, 1)
    leaf_gate = jnp.repeat(leaf_mask, BLOCK)
    gate_par = lax.dynamic_slice_in_dim(leaf_gate[:ORDER], row_index * order_rows, order_rows)
    gate_anc = lax.dynamic_slice_in_dim(leaf_gate[ORDER:], row_index * anc_rows, anc_rows)
    leaf_local = jnp.concatenate(
        [
            leaf_lower_par * gate_par[:, None].astype(jnp.bfloat16),
            leaf_lower_anc * gate_anc[:, None].astype(jnp.bfloat16),
        ],
        axis=0,
    )
    leaf_half = lax.dynamic_slice_in_dim(leaf_local, col_index * col_width, col_width, 1)
    columns = anc_inverse
    product = jnp.dot(
        columns,
        lax.all_gather(lower_half, "row", axis=0, tiled=True),
        preferred_element_type=jnp.float32,
    )
    parent_offdiag = (-product).astype(jnp.bfloat16)
    offdiag_rows = lax.all_gather(parent_offdiag, "col", axis=1, tiled=True)
    columns = lower_one
    diag_sums = lax.psum_scatter(
        lax.dot_general(
            columns, offdiag_rows, (((0,), (0,)), ((), ())), preferred_element_type=jnp.float32
        ),
        "row",
        scatter_dimension=0,
        tiled=True,
    )
    parent_block = parent_pivinv - diag_sums
    parent_round = parent_block.astype(jnp.bfloat16)
    mirrored = lax.all_to_all(offdiag_rows, "row", split_axis=1, concat_axis=0, tiled=True).T
    upper_rows = jnp.concatenate(
        [
            parent_round.reshape(order_rows, row_devices, order_rows),
            mirrored.reshape(order_rows, row_devices, anc_rows),
        ],
        axis=2,
    )
    lower_rows = jnp.concatenate(
        [
            offdiag_rows.reshape(anc_rows, row_devices, order_rows),
            anc_inverse.reshape(anc_rows, row_devices, anc_rows),
        ],
        axis=2,
    )
    inverse_rows = jnp.concatenate(
        [upper_rows.reshape(order_rows, -1), lower_rows.reshape(anc_rows, -1)], axis=0
    )
    columns = inverse_rows
    leaf_product = jnp.dot(
        columns,
        lax.all_gather(leaf_half, "row", axis=0, tiled=True),
        preferred_element_type=jnp.float32,
    )
    leaf_result = (-leaf_product).astype(jnp.bfloat16)
    partial_sums = jnp.sum(leaf_half.astype(jnp.float32) * leaf_result.astype(jnp.float32), axis=0)
    density = leaf_pivots - lax.psum(partial_sums, "row")
    return (
        parent_block,
        parent_offdiag,
        leaf_result[:order_rows],
        leaf_result[order_rows:],
        density,
    )


def solution(mesh):
    placed = (
        P(("pole", "row"), None),
        P(("pole", "row"), None),
        P(("pole", "row"), None),
        P(),
        P(("pole", "row"), None),
        P(("pole", "row"), None),
        P(),
        P(("pole", "col")),
    )
    return jax.shard_map(
        local,
        mesh=mesh,
        in_specs=placed,
        out_specs=(
            P(("pole", "row"), None),
            P(("pole", "row"), "col"),
            P(("pole", "row"), "col"),
            P(("pole", "row"), "col"),
            P(("pole", "col")),
        ),
        check_vma=False,
    )
```

profile of v0, /device:TPU:0, one launch (start us, length us, event | category | flops | bytes accessed | tf_op | source)
XLA Modules:
  0.0 232.6 jit_solution(13250326127232926921)
XLA Ops:
  7.2 0.6 copy-done
  7.8 0.1 broadcast_bitcast_fusion.2
  7.9 0.1 dynamic-slice_convert_fusion.2
  8.0 1.0 broadcast_multiply_fusion.2
  9.0 0.7 constant_dynamic-slice_fusion
  9.8 43.8 %all-gather.3.cloned.1.call-done = bf16[1024,512]{1,0:T(8,128)(2,1)} async-done(((bf16[128,512]{1,0:T(8,128)(2,1)}), bf16[1024,512]{1,0:T(8,128)(2,1)}) %all-gather.3.cloned.1.call-update) | async-done | bytes 1048592 | tf_op jit(solution)/shard_map/all_gather | solution.py:45
  53.6 1.7 fusion.2
  55.3 2.0 all_gather.10
  57.3 2.7 %fusion.10 = f32[1024,1024]{1,0:T(8,128)} fusion(bf16[128,1024]{1,0:T(8,128)(2,1)S(1)} %broadcast_multiply_fusion.2, bf16[128,1024]{0,1:T(8,128)(2,1)S(1)} %all_gather.10), kind=kOutput, calls=%fused_computation.28 | convolution fusion | flops 268435456 | bytes 4718592 | tf_op jit(solution)/shard_map/dot_general | solution.py:52
  60.1 0.6 copy-done.7
  60.7 0.1 fusion.9
  60.8 0.1 broadcast_bitcast_fusion.1
  60.8 0.1 broadcast_bitcast_fusion
  60.9 0.1 dynamic-slice_convert_fusion
  61.0 0.1 broadcast_multiply_fusion
  61.1 0.1 broadcast_multiply_fusion.1
  61.2 0.7 fusion.6
  62.0 0.9 copy.16
  62.8 3.4 %all-to-all-start = ((bf16[128,8,128]{2,0,1:T(8,128)(2,1)}), bf16[128,8,128]{2,0,1:T(8,128)(2,1)S(1)}, u32[]{:S(2)}, u32[]{:S(2)}) async-start(bf16[128,8,128]{2,0,1:T(8,128)(2,1)} %copy.16), calls=%async_computation.1 | async-start | bytes 524288 | tf_op jit(solution)/shard_map/all_to_all | solution.py:61
  66.3 0.2 copy.22
  66.4 0.8 copy.20
  67.3 15.4 %all-to-all-done = bf16[128,8,128]{2,0,1:T(8,128)(2,1)S(1)} async-done(((bf16[128,8,128]{2,0,1:T(8,128)(2,1)}), bf16[128,8,128]{2,0,1:T(8,128)(2,1)S(1)}, u32[]{:S(2)}, u32[]{:S(2)}) %all-to-all-start) | async-done | bytes 262176 | tf_op jit(solution)/shard_map/all_to_all | solution.py:61
  82.7 0.2 copy.17
  82.9 69.2 %reduce-scatter.2.cloned.1.call-done = f32[128,1024]{1,0:T(8,128)} async-done(((f32[1024,1024]{1,0:T(8,128)}), f32[128,1024]{1,0:T(8,128)}) %reduce-scatter.2.cloned.1.call-update) | async-done | bytes 524304 | tf_op jit(solution)/shard_map/reduce_scatter | solution.py:51
  152.1 2.0 convert_bitcast_fusion
  154.1 0.1 pad_maximum_fusion
  154.2 0.4 copy.21
  154.6 48.9 %all-gather.5.cloned.1.call-done = bf16[2048,512]{1,0:T(8,128)(2,1)} async-done(((bf16[256,512]{1,0:T(8,128)(2,1)}), bf16[2048,512]{1,0:T(8,128)(2,1)}) %all-gather.5.cloned.1.call-update) | async-done | bytes 2097168 | tf_op jit(solution)/shard_map/all_gather | solution.py:82
  203.5 2.4 %multiply_reduce_fusion = (f32[512]{0:T(512)S(1)}, bf16[256,512]{1,0:T(8,128)(2,1)S(1)}) fusion(bf16[256,512]{1,0:T(8,128)(2,1)S(1)} %copy-done.2, bf16[2048,512]{1,0:T(8,128)(2,1)} %all-gather.5.cloned.1.call-done, bf16[128,2048]{0,1:T(8,128)(2,1)S(1)} %bitcast.35, bf16[128,2048]{0,1:T(8,128)(2,1)S(1)} %bitcast.36), kind=kOutput, calls=%fused_computation.12 | convolution fusion | flops 539753984 | bytes 3672064 | tf_op jit(solution)/shard_map/dot_general | solution.py:80
  205.9 0.7 fusion.8
  206.6 18.9 %psum.7 = f32[512]{0:T(512)S(1)} all-reduce(f32[512]{0:T(512)S(1)} %get-tuple-element.21), channel_id=1, replica_groups=mesh['pole'=2,'row'=8,'col'=2] {'row'}, use_global_device_ids=true, to_apply=%region_2.0 | all-reduce | flops 512 | bytes 4096 | tf_op jit(solution)/shard_map/psum | solution.py:87
  225.5 0.6 sub.7
  (25 shorter events, 0.3 us)
Async XLA Ops:
  7.2 0.7 copy-start
  7.2 46.4 %all-gather.3.cloned.1.call-start = ((), (), s32[]{:S(2)}) async-start(), calls=%async_computation.2 | async-start | bytes 1179648 | tf_op jit(solution)/shard_map/all_gather | solution.py:45
  9.7 142.3 %reduce-scatter.2.cloned.1.call-start = ((), (), s32[]{:S(2)}) async-start(), calls=%async_computation.3 | async-start | bytes 4718592 | tf_op jit(solution)/shard_map/reduce_scatter | solution.py:51
  60.0 0.7 copy-start.7
  60.0 1.0 copy-start.4
  60.0 1.1 copy-start.5
  60.1 6.2 %copy-start.1 = (bf16[128,1024]{1,0:T(8,128)(2,1)S(1)}, bf16[128,1024]{1,0:T(8,128)(2,1)}, u32[]{:S(2)}) copy-start(bf16[128,1024]{1,0:T(8,128)(2,1)} %param.8) | copy-start | bytes 786436
  60.1 143.4 %all-gather.5.cloned.1.call-start = ((), (), s32[]{:S(2)}) async-start(), calls=%async_computation.4 | async-start | bytes 2359296 | tf_op jit(solution)/shard_map/all_gather | solution.py:82
  61.2 90.9 %copy-start.3 = (f32[128,1024]{1,0:T(8,128)S(1)}, f32[128,1024]{1,0:T(8,128)}, u32[]{:S(2)}) copy-start(f32[128,1024]{1,0:T(8,128)} %param.9) | copy-start | bytes 1572868
  62.8 19.9 %all-to-all-start = ((bf16[128,8,128]{2,0,1:T(8,128)(2,1)}), bf16[128,8,128]{2,0,1:T(8,128)(2,1)S(1)}, u32[]{:S(2)}, u32[]{:S(2)}) async-start(bf16[128,8,128]{2,0,1:T(8,128)(2,1)} %copy.16), calls=%async_computation.1 | async-start | bytes 524288 | tf_op jit(solution)/shard_map/all_to_all | solution.py:61
  82.9 120.6 %copy-start.2 = (bf16[256,512]{1,0:T(8,128)(2,1)S(1)}, bf16[256,512]{1,0:T(8,128)(2,1)}, u32[]{:S(2)}) copy-start(bf16[256,512]{1,0:T(8,128)(2,1)} %fusion.6) | copy-start | bytes 786436
  203.5 22.0 %copy-start.6 = (f32[512]{0:T(512)S(1)}, f32[512]{0:T(512)}, u32[]{:S(2)}) copy-start(f32[512]{0:T(512)} %param.15) | copy-start | bytes 6148
Sparse Core Ops, SparseCore 0:
  10.7 42.8 all-gather.2
  60.2 91.8 reduce-scatter.1
  154.4 49.0 all-gather.4
where the time goes:
time: 233 us
  waiting for transfers between devices  177 us (76%)
  blocking collectives  20.9 us (9%)
  between operations  13.9 us (6%)
  matrix products  6.8 us (3%)
  local copies, waits for them, and re-layouts  5.36 us (2%)
  other arithmetic  4.75 us (2%)
  starting transfers between devices  3.53 us (2%)
    reduce_scatter x1, waiting for transfers between devices, local(): lax.psum_scatter(lax.dot_general(columns, offdiag_rows, (((0,), (0,)), ((...  69.2 us
    all_gather x1, waiting for transfers between devices, local(): lax.all_gather(leaf_half, 'row', axis=0, tiled=True)  48.9 us
    all_gather x1, waiting for transfers between devices, local(): lax.all_gather(lower_half, 'row', axis=0, tiled=True)  43.8 us
    psum x1, blocking collectives, local(): density = leaf_pivots - lax.psum(partial_sums, 'row')  18.9 us
    all_to_all x1, waiting for transfers between devices, local(): lax.all_to_all(offdiag_rows, 'row', split_axis=1, concat_axis=0, tiled=True)  15.4 us
  transfers between devices with their start and end apart: 4, of which 4 were waited for; matrix products, arithmetic and copies ran while one was open for 2% of the time, Pallas kernels for 0%

commit v1 on v0

--- a/solution.py
+++ b/solution.py
@@ -94,6 +94,89 @@
     )
 
 
+def gathered_rows(pieces):
+    widths = [p.shape[1] for p in pieces]
+    full = lax.all_gather(jnp.concatenate(pieces, axis=1), ("row", "col"), axis=0, tiled=True)
+    out, at = [], 0
+    for w in widths:
+        out.append(full[:, at : at + w])
+        at += w
+    return out
+
+
+def local_whole(
+    anc_inverse,
+    parent_pivinv,
+    parent_lower,
+    parent_mask,
+    leaf_lower_par,
+    leaf_lower_anc,
+    leaf_mask,
+    leaf_pivots,
+):
+    row_index = lax.axis_index("row")
+    row_devices = lax.axis_size("row")
+    col_index = lax.axis_index("col")
+    anc_rows = anc_inverse.shape[0]
+    order_rows = parent_pivinv.shape[0]
+    col_width = leaf_pivots.shape[0]
+    off_width = parent_lower.shape[1] // 2
+    half = anc_rows // 2
+
+    def mine(x):
+        return lax.dynamic_slice_in_dim(x, col_index * half, half, 0)
+
+    anc_full, lower_full, par_full, anc_leaf_full = gathered_rows(
+        [mine(anc_inverse), mine(parent_lower), mine(leaf_lower_par), mine(leaf_lower_anc)]
+    )
+    order_all = order_rows * row_devices
+    parent_gate = jnp.repeat(parent_mask, BLOCK).astype(jnp.bfloat16)
+    leaf_gate = jnp.repeat(leaf_mask, BLOCK).astype(jnp.bfloat16)
+    lower_m = lower_full * parent_gate[:, None]
+    par_m = par_full * leaf_gate[:order_all, None]
+    anc_m = anc_leaf_full * leaf_gate[order_all:, None]
+
+    offdiag_all = (-jnp.dot(anc_full, lower_m, preferred_element_type=jnp.float32)).astype(jnp.bfloat16)
+    lower_cols = lax.dynamic_slice_in_dim(lower_m, row_index * order_rows, order_rows, 1)
+    parent_block = parent_pivinv - lax.dot_general(
+        lower_cols, offdiag_all, (((0,), (0,)), ((), ())), preferred_element_type=jnp.float32
+    )
+    parent_round = parent_block.astype(jnp.bfloat16)
+
+    par_half = lax.dynamic_slice_in_dim(par_m, col_index * col_width, col_width, 1)
+    anc_half = lax.dynamic_slice_in_dim(anc_m, col_index * col_width, col_width, 1)
+    offdiag_cols = lax.dynamic_slice_in_dim(offdiag_all, row_index * order_rows, order_rows, 1)
+    offdiag_rows = lax.dynamic_slice_in_dim(offdiag_all, row_index * anc_rows, anc_rows, 0)
+    upper_sum = jnp.dot(parent_round, par_half, preferred_element_type=jnp.float32) + lax.dot_general(
+        offdiag_cols, anc_half, (((0,), (0,)), ((), ())), preferred_element_type=jnp.float32
+    )
+    lower_sum = jnp.dot(offdiag_rows, par_half, preferred_element_type=jnp.float32) + jnp.dot(
+        anc_inverse, anc_half, preferred_element_type=jnp.float32
+    )
+    leaf_par_block = (-upper_sum).astype(jnp.bfloat16)
+    leaf_anc_block = (-lower_sum).astype(jnp.bfloat16)
+
+    par_own = lax.dynamic_slice_in_dim(par_half, row_index * order_rows, order_rows, 0)
+    anc_own = lax.dynamic_slice_in_dim(anc_half, row_index * anc_rows, anc_rows, 0)
+    partial_sums = jnp.sum(
+        par_own.astype(jnp.float32) * leaf_par_block.astype(jnp.float32), axis=0
+    ) + jnp.sum(anc_own.astype(jnp.float32) * leaf_anc_block.astype(jnp.float32), axis=0)
+    spread = jnp.broadcast_to(partial_sums[None], (row_devices, col_width))
+    column_sums = jnp.sum(lax.all_to_all(spread, "row", 0, 0, tiled=True), axis=0)
+    density = leaf_pivots - column_sums
+    offdiag_own = lax.dynamic_slice_in_dim(offdiag_rows, col_index * off_width, off_width, 1)
+    return parent_block, offdiag_own, leaf_par_block, leaf_anc_block, density
+
+
+def fits_whole(mesh, anc_rows, order_rows):
+    anc_all = anc_rows * mesh.shape["row"]
+    return (
+        anc_rows == order_rows
+        and anc_rows % 2 == 0
+        and anc_all * anc_all * 2 <= 16 * 1024 * 1024
+    )
+
+
 def solution(mesh):
     placed = (
         P(("pole", "row"), None),
@@ -105,16 +188,21 @@
         P(),
         P(("pole", "col")),
     )
-    return jax.shard_map(
-        local,
-        mesh=mesh,
-        in_specs=placed,
-        out_specs=(
-            P(("pole", "row"), None),
-            P(("pole", "row"), "col"),
-            P(("pole", "row"), "col"),
-            P(("pole", "row"), "col"),
-            P(("pole", "col")),
-        ),
-        check_vma=False,
-    )
+    placed_out = (
+        P(("pole", "row"), None),
+        P(("pole", "row"), "col"),
+        P(("pole", "row"), "col"),
+        P(("pole", "row"), "col"),
+        P(("pole", "col")),
+    )
+    shards = mesh.shape["pole"] * mesh.shape["row"]
+
+    def run(*args):
+        anc_rows = args[0].shape[0] // shards
+        order_rows = args[1].shape[0] // shards
+        body = local_whole if fits_whole(mesh, anc_rows, order_rows) else local
+        return jax.shard_map(
+            body, mesh=mesh, in_specs=placed, out_specs=placed_out, check_vma=False
+        )(*args)
+
+    return run

time: 233 us -> 117 us (0.50)
  waiting for transfers between devices: 177 us -> 83.8 us
  blocking collectives: 20.9 us -> 0 us
    reduce_scatter x1 -> x0, waiting for transfers between devices: 69.2 us -> none  [local(): lax.psum_scatter(lax.dot_general(columns, offdiag_rows, (((0,), (0,)), ((...]
    psum x1 -> x0, blocking collectives: 18.9 us -> none  [local(): density = leaf_pivots - lax.psum(partial_sums, 'row')]
    all_gather x2 -> x1, waiting for transfers between devices: 92.7 us -> 78 us  [gathered_rows(): lax.all_gather(jnp.concatenate(pieces, axis=1), ('row', 'col'), axis=0, t...]
    all_to_all x1, waiting for transfers between devices: 15.4 us -> 5.73 us  [local_whole(): lax.all_to_all(spread, 'row', 0, 0, tiled=True)]
    dot_general x3 -> x6, matrix products: 6.8 us -> 7.24 us  [the longest x1 4.01 us: local_whole(): jnp.dot(anc_full, lower_m, preferred_element_type=jnp.float32)]
  transfers between devices with their start and end apart: 4 -> 2, of which waited for: 4 -> 2; matrix products, arithmetic and copies ran while one was open for 2% -> 1% of each run, Pallas kernels for 0% -> 0%
where the time goes in v1:
time: 117 us
  waiting for transfers between devices  83.8 us (72%)
  between operations  14.2 us (12%)
  matrix products  7.24 us (6%)
  other arithmetic  4.7 us (4%)
  local copies, waits for them, and re-layouts  3.73 us (3%)
  starting transfers between devices  3.34 us (3%)
    all_gather x1, waiting for transfers between devices, gathered_rows(): lax.all_gather(jnp.concatenate(pieces, axis=1), ('row', 'col'), axis=0, t...  78 us
    all_to_all x1, waiting for transfers between devices, local_whole(): lax.all_to_all(spread, 'row', 0, 0, tiled=True)  5.73 us
    dot_general x1, matrix products, local_whole(): jnp.dot(anc_full, lower_m, preferred_element_type=jnp.float32)  4.01 us
    all_to_all x1, starting transfers between devices, local_whole(): lax.all_to_all(spread, 'row', 0, 0, tiled=True)  3.31 us
    mul x1, other arithmetic, local_whole(): anc_m = anc_leaf_full * leaf_gate[order_all:, None]  3.24 us
  transfers between devices with their start and end apart: 2, of which 2 were waited for; matrix products, arithmetic and copies ran while one was open for 1% of the time, Pallas kernels for 0%

profile of v1, /device:TPU:0, one launch (start us, length us, event | category | flops | bytes accessed | tf_op | source)
XLA Modules:
  0.0 117.0 jit_solution(18202725463987624907)
XLA Ops:
  7.2 0.0 copy-start.4
  7.2 0.0 copy-start.5
  7.2 0.0 all-gather.2.cloned.1.call-start
  7.2 1.0 constant_dynamic-slice_fusion
  8.2 1.0 constant_dynamic-slice_fusion.2
  9.2 0.8 pad_maximum_fusion
  10.1 0.0 all-gather.2.cloned.1.call-update
  10.1 0.0 copy-done.4
  10.1 0.1 fusion.21
  10.2 0.1 broadcast_bitcast_fusion
  10.3 0.0 copy-done.5
  10.3 0.1 broadcast_bitcast_fusion.2
  10.4 78.0 %all-gather.2.cloned.1.call-done = bf16[1024,4096]{1,0:T(8,128)(2,1)} async-done(((bf16[64,4096]{1,0:T(8,128)(2,1)}), bf16[1024,4096]{1,0:T(8,128)(2,1)}) %all-gather.2.cloned.1.call-update) | async-done | bytes 8388624 | tf_op jit(solution)/shard_map/all_gather | solution.py:99
  88.4 3.2 %slice_multiply_fusion = (bf16[1024,1024]{1,0:T(8,128)(2,1)S(1)}, bf16[1024,1024]{1,0:T(8,128)(2,1)S(1)}, bf16[1024,1024]{1,0:T(8,128)(2,1)S(1)}) fusion(bf16[1024,4096]{1,0:T(8,128)(2,1)} %all-gather.2.cloned.1.call-done, bf16[1024]{0:T(1024)(128)(2,1)S(1)} %bitcast.21, bf16[1024]{0:T(1024)(128)(2,1)S(1)} %bitcast.20, bf16[1024]{0:T(1024)(128)(2,1)S(1)} %bitcast.22), kind=kLoop, calls=%fused_computation.1 | loop fusion | flops 3145728 | bytes 12589056 | tf_op jit(solution)/shard_map/mul | solution.py:137
  91.6 0.0 copy-start.2
  91.7 4.0 %negate_convert_fusion = bf16[1024,1024]{1,0:T(8,128)(2,1)S(1)} fusion(bf16[1024,1024]{1,0:T(8,128)(2,1)S(1)} %get-tuple-element.7, bf16[1024,4096]{1,0:T(8,128)(2,1)} %all-gather.2.cloned.1.call-done), kind=kOutput, calls=%fused_computation | convolution fusion | flops 2149580800 | bytes 6291456 | tf_op jit(solution)/shard_map/dot_general | solution.py:139
  95.7 0.3 fusion.8
  96.0 0.0 copy-done.2
  96.0 0.0 copy-start.1
  96.0 0.5 convolution_subtract_fusion
  96.5 0.0 copy-start
  96.5 0.3 fusion.10
  96.9 0.0 copy-start.3
  96.9 0.1 copy-done.1
  97.0 1.0 multiply_reduce_fusion
  98.0 1.1 multiply_reduce_fusion.1
  99.1 0.0 copy-done
  99.1 0.6 broadcast_in_dim.20
  99.7 3.3 %all-to-all-start = ((f32[8,1,512]{2,1,0:T(1,128)}), f32[8,1,512]{2,1,0:T(1,128)S(1)}, u32[]{:S(2)}, u32[]{:S(2)}) async-start(f32[8,1,512]{2,1,0:T(1,128)} %broadcast_in_dim.20), calls=%async_computation | async-start | bytes 32768 | tf_op jit(solution)/shard_map/all_to_all | solution.py:165
  103.0 0.8 dynamic_slice.41
  103.8 5.7 %all-to-all-done = f32[8,1,512]{2,1,0:T(1,128)S(1)} async-done(((f32[8,1,512]{2,1,0:T(1,128)}), f32[8,1,512]{2,1,0:T(1,128)S(1)}, u32[]{:S(2)}, u32[]{:S(2)}) %all-to-all-start) | async-done | bytes 16416 | tf_op jit(solution)/shard_map/all_to_all | solution.py:165
  109.5 0.6 sub.7
  (8 shorter events, 0.1 us)
Async XLA Ops:
  7.2 2.9 %copy-start.4 = (s32[8]{0:T(128)S(1)}, s32[8]{0:T(128)}, u32[]{:S(2)}) copy-start(s32[8]{0:T(128)} %param.14) | copy-start | bytes 100
  7.2 3.1 %copy-start.5 = (s32[4]{0:T(128)S(1)}, s32[4]{0:T(128)}, u32[]{:S(2)}) copy-start(s32[4]{0:T(128)} %param.11) | copy-start | bytes 52
  7.2 81.2 %all-gather.2.cloned.1.call-start = ((), (), s32[]{:S(2)}) async-start(), calls=%async_computation.1 | async-start | bytes 8912896 | tf_op jit(solution)/shard_map/all_gather | solution.py:99
  91.6 4.4 %copy-start.2 = (f32[128,1024]{1,0:T(8,128)S(1)}, f32[128,1024]{1,0:T(8,128)}, u32[]{:S(2)}) copy-start(f32[128,1024]{1,0:T(8,128)} %param.9) | copy-start | bytes 1572868
  96.0 1.0 copy-start.1
  96.5 2.5 %copy-start = (f32[128,1024]{1,0:T(8,128)}, f32[128,1024]{1,0:T(8,128)S(1)}, u32[]{:S(2)}) copy-start(f32[128,1024]{1,0:T(8,128)S(1)} %convolution_subtract_fusion) | copy-start | bytes 1572868
  96.9 12.7 %copy-start.3 = (f32[512]{0:T(512)S(1)}, f32[512]{0:T(512)}, u32[]{:S(2)}) copy-start(f32[512]{0:T(512)} %param.15) | copy-start | bytes 6148
  99.7 9.8 %all-to-all-start = ((f32[8,1,512]{2,1,0:T(1,128)}), f32[8,1,512]{2,1,0:T(1,128)S(1)}, u32[]{:S(2)}, u32[]{:S(2)}) async-start(f32[8,1,512]{2,1,0:T(1,128)} %broadcast_in_dim.20), calls=%async_computation | async-start | bytes 32768 | tf_op jit(solution)/shard_map/all_to_all | solution.py:165
Sparse Core Ops, SparseCore 0:
  10.8 77.5 all-gather.1

commit v2 on v1

--- a/solution.py
+++ b/solution.py
@@ -94,16 +94,6 @@
     )
 
 
-def gathered_rows(pieces):
-    widths = [p.shape[1] for p in pieces]
-    full = lax.all_gather(jnp.concatenate(pieces, axis=1), ("row", "col"), axis=0, tiled=True)
-    out, at = [], 0
-    for w in widths:
-        out.append(full[:, at : at + w])
-        at += w
-    return out
-
-
 def local_whole(
     anc_inverse,
     parent_pivinv,
@@ -126,15 +116,24 @@
     def mine(x):
         return lax.dynamic_slice_in_dim(x, col_index * half, half, 0)
 
-    anc_full, lower_full, par_full, anc_leaf_full = gathered_rows(
-        [mine(anc_inverse), mine(parent_lower), mine(leaf_lower_par), mine(leaf_lower_anc)]
-    )
     order_all = order_rows * row_devices
     parent_gate = jnp.repeat(parent_mask, BLOCK).astype(jnp.bfloat16)
     leaf_gate = jnp.repeat(leaf_mask, BLOCK).astype(jnp.bfloat16)
-    lower_m = lower_full * parent_gate[:, None]
-    par_m = par_full * leaf_gate[:order_all, None]
-    anc_m = anc_leaf_full * leaf_gate[order_all:, None]
+    anc_start = row_index * anc_rows + col_index * half
+    order_start = row_index * order_rows + col_index * half
+    lower_gate = lax.dynamic_slice_in_dim(parent_gate, anc_start, half)
+    par_gate = lax.dynamic_slice_in_dim(leaf_gate[:order_all], order_start, half)
+    anc_gate = lax.dynamic_slice_in_dim(leaf_gate[order_all:], anc_start, half)
+    stacked = jnp.stack(
+        [
+            mine(anc_inverse),
+            mine(parent_lower) * lower_gate[:, None],
+            mine(leaf_lower_par) * par_gate[:, None],
+            mine(leaf_lower_anc) * anc_gate[:, None],
+        ]
+    )
+    full = lax.all_gather(stacked, ("row", "col"), axis=1, tiled=True)
+    anc_full, lower_m, par_m, anc_m = full[0], full[1], full[2], full[3]
 
     offdiag_all = (-jnp.dot(anc_full, lower_m, preferred_element_type=jnp.float32)).astype(jnp.bfloat16)
     lower_cols = lax.dynamic_slice_in_dim(lower_m, row_index * order_rows, order_rows, 1)
@@ -168,11 +167,12 @@
     return parent_block, offdiag_own, leaf_par_block, leaf_anc_block, density
 
 
-def fits_whole(mesh, anc_rows, order_rows):
+def fits_whole(mesh, anc_rows, order_rows, order_cols, leaf_cols):
     anc_all = anc_rows * mesh.shape["row"]
     return (
         anc_rows == order_rows
         and anc_rows % 2 == 0
+        and len({anc_all, order_cols, leaf_cols}) == 1
         and anc_all * anc_all * 2 <= 16 * 1024 * 1024
     )
 
@@ -200,7 +200,7 @@
     def run(*args):
         anc_rows = args[0].shape[0] // shards
         order_rows = args[1].shape[0] // shards
-        body = local_whole if fits_whole(mesh, anc_rows, order_rows) else local
+        body = local_whole if fits_whole(mesh, anc_rows, order_rows, args[2].shape[1], args[4].shape[1]) else local
         return jax.shard_map(
             body, mesh=mesh, in_specs=placed, out_specs=placed_out, check_vma=False
         )(*args)

time: 117 us -> 119 us (1.017)
  local copies, waits for them, and re-layouts: 3.73 us -> 7.3 us
  matrix products: 7.24 us -> 5.52 us
    slice x1 -> x2, local copies, waits for them, and re-layouts: 0.07 us -> 3.83 us  [the longest x1 3.75 us: local_whole(): anc_full, lower_m, par_m, anc_m = (full[0], full[1], full[2], full[3])]
    mul x1 -> x0, other arithmetic: 3.24 us -> none  [local_whole(): anc_m = anc_leaf_full * leaf_gate[order_all:, None]]
    another operation x0 -> x3, other arithmetic: none -> 3 us  [local_whole(): jnp.stack([mine(anc_inverse), mine(parent_lower) * lower_gate[:, None], m...]
    dynamic_slice x2 -> x3, local copies, waits for them, and re-layouts: 1.98 us -> 0.23 us  [the longest x1 0.08 us: local_whole(): lower_gate = lax.dynamic_slice_in_dim(parent_gate, anc_start, half)]
    dot_general x1, matrix products: 4.01 us -> 2.33 us  [local_whole(): jnp.dot(anc_full, lower_m, preferred_element_type=jnp.float32)]
    unnamed x17 -> x16, local copies, waits for them, and re-layouts: 0.28 us -> 1.85 us
where the time goes in v2:
time: 119 us
  waiting for transfers between devices  83.5 us (70%)
  between operations  14.2 us (12%)
  local copies, waits for them, and re-layouts  7.3 us (6%)
  matrix products  5.52 us (5%)
  other arithmetic  4.94 us (4%)
  starting transfers between devices  3.36 us (3%)
    all_gather x1, waiting for transfers between devices, local_whole(): full = lax.all_gather(stacked, ('row', 'col'), axis=1, tiled=True)  77.8 us
    all_to_all x1, waiting for transfers between devices, local_whole(): lax.all_to_all(spread, 'row', 0, 0, tiled=True)  5.73 us
    slice x1, local copies, waits for them, and re-layouts, local_whole(): anc_full, lower_m, par_m, anc_m = (full[0], full[1], full[2], full[3])  3.75 us
    all_to_all x1, starting transfers between devices, local_whole(): lax.all_to_all(spread, 'row', 0, 0, tiled=True)  3.32 us
    another operation x3, other arithmetic, local_whole(): jnp.stack([mine(anc_inverse), mine(parent_lower) * lower_gate[:, None], m...  3 us
  transfers between devices with their start and end apart: 2, of which 2 were waited for; matrix products, arithmetic and copies ran while one was open for 1% of the time, Pallas kernels for 0%

profile of v2, /device:TPU:0, one launch (start us, length us, event | category | flops | bytes accessed | tf_op | source)
XLA Modules:
  0.0 118.8 jit_solution(13952267705256480365)
XLA Ops:
  7.2 0.0 all-gather.2.cloned.1.call-start
  7.2 0.7 convert_element_type.44
  7.9 0.1 fusion.30
  8.0 0.1 broadcast_bitcast_fusion.1
  8.0 0.1 broadcast_bitcast_fusion
  8.1 0.1 dynamic_slice.55
  8.2 0.1 dynamic_slice.57
  8.3 0.7 convert_element_type.42
  8.9 0.1 broadcast_bitcast_fusion.2
  9.0 0.1 dynamic_slice.53
  9.1 1.1 multiply_bitcast_fusion.2
  10.1 1.1 multiply_bitcast_fusion
  11.2 0.9 pad_maximum_fusion
  12.1 0.0 all-gather.2.cloned.1.call-update
  12.1 77.8 %all-gather.2.cloned.1.call-done = bf16[4,1024,1024]{2,1,0:T(8,128)(2,1)} async-done(((bf16[4,64,1024]{2,1,0:T(8,128)(2,1)}), bf16[4,1024,1024]{2,1,0:T(8,128)(2,1)}) %all-gather.2.cloned.1.call-update) | async-done | bytes 8388624 | tf_op jit(solution)/shard_map/all_gather | solution.py:135
  89.9 3.8 %fusion.29 = (bf16[1,1024,1024]{2,1,0:T(8,128)(2,1)S(1)}, bf16[1,1024,1024]{2,1,0:T(8,128)(2,1)S(1)}, bf16[1,1024,1024]{2,1,0:T(8,128)(2,1)S(1)}) fusion(bf16[4,1024,1024]{2,1,0:T(8,128)(2,1)} %all-gather.2.cloned.1.call-done), kind=kLoop, calls=%fused_computation.44 | loop fusion | bytes 12582912 | tf_op jit(solution)/shard_map/slice | solution.py:136
  93.7 1.5 %copy-done = bf16[4,1024,1024]{2,1,0:T(8,128)(2,1)S(1)} copy-done((bf16[4,1024,1024]{2,1,0:T(8,128)(2,1)S(1)}, bf16[4,1024,1024]{2,1,0:T(8,128)(2,1)}, u32[]{:S(2)}) %copy-start) | copy-done | bytes 8388632
  95.2 2.3 %negate_convert_fusion = bf16[1024,1024]{1,0:T(8,128)(2,1)S(1)} fusion(bf16[4,1024,1024]{2,1,0:T(8,128)(2,1)S(1)} %copy-done), kind=kOutput, calls=%fused_computation | convolution fusion | flops 2149580800 | bytes 6291456 | tf_op jit(solution)/shard_map/dot_general | solution.py:138
  97.5 0.3 fusion.8
  97.8 0.0 copy-start.2
  97.8 0.5 convolution_subtract_fusion
  98.3 0.0 copy-start.1
  98.3 0.3 fusion.10
  98.7 0.0 copy-start.4
  98.7 0.1 copy-done.2
  98.8 1.0 fusion.16
  99.8 1.1 fusion.17
  100.9 0.6 broadcast_in_dim.20
  101.5 3.3 %all-to-all-start = ((f32[8,1,512]{2,1,0:T(1,128)}), f32[8,1,512]{2,1,0:T(1,128)S(1)}, u32[]{:S(2)}, u32[]{:S(2)}) async-start(f32[8,1,512]{2,1,0:T(1,128)} %broadcast_in_dim.20), calls=%async_computation | async-start | bytes 32768 | tf_op jit(solution)/shard_map/all_to_all | solution.py:164
  104.8 0.8 dynamic_slice.60
  105.6 5.7 %all-to-all-done = f32[8,1,512]{2,1,0:T(1,128)S(1)} async-done(((f32[8,1,512]{2,1,0:T(1,128)}), f32[8,1,512]{2,1,0:T(1,128)S(1)}, u32[]{:S(2)}, u32[]{:S(2)}) %all-to-all-start) | async-done | bytes 16416 | tf_op jit(solution)/shard_map/all_to_all | solution.py:164
  111.3 0.6 sub.7
  (10 shorter events, 0.1 us)
Async XLA Ops:
  7.2 82.7 %all-gather.2.cloned.1.call-start = ((), (), s32[]{:S(2)}) async-start(), calls=%async_computation.1 | async-start | bytes 8912896 | tf_op jit(solution)/shard_map/all_gather | solution.py:135
  89.9 5.2 %copy-start = (bf16[4,1024,1024]{2,1,0:T(8,128)(2,1)S(1)}, bf16[4,1024,1024]{2,1,0:T(8,128)(2,1)}, u32[]{:S(2)}) copy-start(bf16[4,1024,1024]{2,1,0:T(8,128)(2,1)} %all-gather.2.cloned.1.call-done) | copy-start | bytes 25165828
  95.1 2.7 %copy-start.3 = (f32[128,1024]{1,0:T(8,128)S(1)}, f32[128,1024]{1,0:T(8,128)}, u32[]{:S(2)}) copy-start(f32[128,1024]{1,0:T(8,128)} %param.9) | copy-start | bytes 1572868
  97.8 1.0 copy-start.2
  98.3 2.5 %copy-start.1 = (f32[128,1024]{1,0:T(8,128)}, f32[128,1024]{1,0:T(8,128)S(1)}, u32[]{:S(2)}) copy-start(f32[128,1024]{1,0:T(8,128)S(1)} %convolution_subtract_fusion) | copy-start | bytes 1572868
  98.7 12.7 %copy-start.4 = (f32[512]{0:T(512)S(1)}, f32[512]{0:T(512)}, u32[]{:S(2)}) copy-start(f32[512]{0:T(512)} %param.15) | copy-start | bytes 6148
  101.5 9.8 %all-to-all-start = ((f32[8,1,512]{2,1,0:T(1,128)}), f32[8,1,512]{2,1,0:T(1,128)S(1)}, u32[]{:S(2)}, u32[]{:S(2)}) async-start(f32[8,1,512]{2,1,0:T(1,128)} %broadcast_in_dim.20), calls=%async_computation | async-start | bytes 32768 | tf_op jit(solution)/shard_map/all_to_all | solution.py:164
Sparse Core Ops, SparseCore 0:
  12.2 77.6 all-gather.1

commit v3 on v2

--- a/solution.py
+++ b/solution.py
@@ -135,17 +135,20 @@
     full = lax.all_gather(stacked, ("row", "col"), axis=1, tiled=True)
     anc_full, lower_m, par_m, anc_m = full[0], full[1], full[2], full[3]
 
-    offdiag_all = (-jnp.dot(anc_full, lower_m, preferred_element_type=jnp.float32)).astype(jnp.bfloat16)
     lower_cols = lax.dynamic_slice_in_dim(lower_m, row_index * order_rows, order_rows, 1)
+    offdiag_cols = (-jnp.dot(anc_full, lower_cols, preferred_element_type=jnp.float32)).astype(
+        jnp.bfloat16
+    )
+    offdiag_rows = (-jnp.dot(anc_inverse, lower_m, preferred_element_type=jnp.float32)).astype(
+        jnp.bfloat16
+    )
     parent_block = parent_pivinv - lax.dot_general(
-        lower_cols, offdiag_all, (((0,), (0,)), ((), ())), preferred_element_type=jnp.float32
+        offdiag_cols, lower_m, (((0,), (0,)), ((), ())), preferred_element_type=jnp.float32
     )
     parent_round = parent_block.astype(jnp.bfloat16)
 
     par_half = lax.dynamic_slice_in_dim(par_m, col_index * col_width, col_width, 1)
     anc_half = lax.dynamic_slice_in_dim(anc_m, col_index * col_width, col_width, 1)
-    offdiag_cols = lax.dynamic_slice_in_dim(offdiag_all, row_index * order_rows, order_rows, 1)
-    offdiag_rows = lax.dynamic_slice_in_dim(offdiag_all, row_index * anc_rows, anc_rows, 0)
     upper_sum = jnp.dot(parent_round, par_half, preferred_element_type=jnp.float32) + lax.dot_general(
         offdiag_cols, anc_half, (((0,), (0,)), ((), ())), preferred_element_type=jnp.float32
     )

time: 119 us -> 118 us (level)
    dot_general x2 -> x3, matrix products: 2.81 us -> 1.95 us  [the longest x1 0.76 us: local_whole(): jnp.dot(anc_inverse, lower_m, preferred_element_type=jnp.float32)]
    unnamed x16 -> x17, local copies, waits for them, and re-layouts: 1.85 us -> 2.63 us
where the time goes in v3:
time: 118 us
  waiting for transfers between devices  83.5 us (71%)
  between operations  14.2 us (12%)
  local copies, waits for them, and re-layouts  7.32 us (6%)
  other arithmetic  4.94 us (4%)
  matrix products  4.65 us (4%)
  starting transfers between devices  3.36 us (3%)
    all_gather x1, waiting for transfers between devices, local_whole(): full = lax.all_gather(stacked, ('row', 'col'), axis=1, tiled=True)  77.8 us
    all_to_all x1, waiting for transfers between devices, local_whole(): lax.all_to_all(spread, 'row', 0, 0, tiled=True)  5.71 us
    slice x1, local copies, waits for them, and re-layouts, local_whole(): anc_full, lower_m, par_m, anc_m = (full[0], full[1], full[2], full[3])  3.75 us
    all_to_all x1, starting transfers between devices, local_whole(): lax.all_to_all(spread, 'row', 0, 0, tiled=True)  3.32 us
    another operation x3, other arithmetic, local_whole(): jnp.stack([mine(anc_inverse), mine(parent_lower) * lower_gate[:, None], m...  3 us
    unnamed x17, local copies, waits for them, and re-layouts  2.63 us
  transfers between devices with their start and end apart: 2, of which 2 were waited for; matrix products, arithmetic and copies ran while one was open for 1% of the time, Pallas kernels for 0%

profile of v3, /device:TPU:0, one launch (start us, length us, event | category | flops | bytes accessed | tf_op | source)
XLA Modules:
  0.0 117.9 jit_solution(16154111242631379087)
XLA Ops:
  7.2 0.0 all-gather.2.cloned.1.call-start
  7.2 0.7 convert_element_type.48
  7.9 0.1 fusion.44
  8.0 0.1 broadcast_bitcast_fusion
  8.0 0.1 broadcast_bitcast_fusion.1
  8.1 0.1 dynamic_slice.51
  8.2 0.1 dynamic_slice.49
  8.3 0.7 convert_element_type.46
  8.9 0.1 broadcast_bitcast_fusion.2
  9.0 0.1 dynamic_slice.47
  9.1 1.1 multiply_bitcast_fusion.2
  10.1 1.1 multiply_bitcast_fusion
  11.2 0.9 pad_maximum_fusion
  12.1 0.0 all-gather.2.cloned.1.call-update
  12.1 77.8 %all-gather.2.cloned.1.call-done = bf16[4,1024,1024]{2,1,0:T(8,128)(2,1)} async-done(((bf16[4,64,1024]{2,1,0:T(8,128)(2,1)}), bf16[4,1024,1024]{2,1,0:T(8,128)(2,1)}) %all-gather.2.cloned.1.call-update) | async-done | bytes 8388624 | tf_op jit(solution)/shard_map/all_gather | solution.py:135
  89.9 3.8 %fusion.43 = (bf16[1,1024,1024]{2,1,0:T(8,128)(2,1)S(1)}, bf16[1,1024,1024]{2,1,0:T(8,128)(2,1)S(1)}, bf16[1,1024,1024]{2,1,0:T(8,128)(2,1)S(1)}) fusion(bf16[4,1024,1024]{2,1,0:T(8,128)(2,1)} %all-gather.2.cloned.1.call-done), kind=kLoop, calls=%fused_computation.51 | loop fusion | bytes 12582912 | tf_op jit(solution)/shard_map/slice | solution.py:136
  93.7 1.5 %copy-done = bf16[4,1024,1024]{2,1,0:T(8,128)(2,1)S(1)} copy-done((bf16[4,1024,1024]{2,1,0:T(8,128)(2,1)S(1)}, bf16[4,1024,1024]{2,1,0:T(8,128)(2,1)}, u32[]{:S(2)}) %copy-start) | copy-done | bytes 8388632
  95.1 0.7 fusion.12
  95.9 0.0 copy-start.2
  95.9 0.5 fusion.9
  96.4 0.0 copy-start.1
  96.4 0.3 fusion.25
  96.7 0.1 copy-done.2
  96.8 0.8 fusion.13
  97.6 0.3 fusion.23
  98.0 1.0 fusion.32
  99.0 1.0 fusion.31
  100.0 0.6 broadcast_in_dim.20
  100.6 3.3 %all-to-all-start = ((f32[8,1,512]{2,1,0:T(1,128)}), f32[8,1,512]{2,1,0:T(1,128)S(1)}, u32[]{:S(2)}, u32[]{:S(2)}) async-start(f32[8,1,512]{2,1,0:T(1,128)} %broadcast_in_dim.20), calls=%async_computation | async-start | bytes 32768 | tf_op jit(solution)/shard_map/all_to_all | solution.py:167
  104.0 0.8 copy.16
  104.8 5.7 %all-to-all-done = f32[8,1,512]{2,1,0:T(1,128)S(1)} async-done(((f32[8,1,512]{2,1,0:T(1,128)}), f32[8,1,512]{2,1,0:T(1,128)S(1)}, u32[]{:S(2)}, u32[]{:S(2)}) %all-to-all-start) | async-done | bytes 16416 | tf_op jit(solution)/shard_map/all_to_all | solution.py:167
  110.5 0.6 sub.7
  (12 shorter events, 0.1 us)
Async XLA Ops:
  7.2 82.7 %all-gather.2.cloned.1.call-start = ((), (), s32[]{:S(2)}) async-start(), calls=%async_computation.1 | async-start | bytes 8912896 | tf_op jit(solution)/shard_map/all_gather | solution.py:135
  89.9 5.2 %copy-start = (bf16[4,1024,1024]{2,1,0:T(8,128)(2,1)S(1)}, bf16[4,1024,1024]{2,1,0:T(8,128)(2,1)}, u32[]{:S(2)}) copy-start(bf16[4,1024,1024]{2,1,0:T(8,128)(2,1)} %all-gather.2.cloned.1.call-done) | copy-start | bytes 25165828
  93.7 2.2 %copy-start.3 = (f32[128,1024]{1,0:T(8,128)S(1)}, f32[128,1024]{1,0:T(8,128)}, u32[]{:S(2)}) copy-start(f32[128,1024]{1,0:T(8,128)} %param.9) | copy-start | bytes 1572868
  95.9 1.0 copy-start.2
  96.4 1.2 %copy-start.1 = (f32[128,1024]{1,0:T(8,128)}, f32[128,1024]{1,0:T(8,128)S(1)}, u32[]{:S(2)}) copy-start(f32[128,1024]{1,0:T(8,128)S(1)} %fusion.9) | copy-start | bytes 1572868
  98.0 12.6 %copy-start.4 = (f32[512]{0:T(512)S(1)}, f32[512]{0:T(512)}, u32[]{:S(2)}) copy-start(f32[512]{0:T(512)} %param.15) | copy-start | bytes 6148
  100.6 9.8 %all-to-all-start = ((f32[8,1,512]{2,1,0:T(1,128)}), f32[8,1,512]{2,1,0:T(1,128)S(1)}, u32[]{:S(2)}, u32[]{:S(2)}) async-start(f32[8,1,512]{2,1,0:T(1,128)} %broadcast_in_dim.20), calls=%async_computation | async-start | bytes 32768 | tf_op jit(solution)/shard_map/all_to_all | solution.py:167
Sparse Core Ops, SparseCore 0:
  12.2 77.6 all-gather.1

commit v4 on v1

--- a/solution.py
+++ b/solution.py
@@ -1,6 +1,8 @@
 import jax
 import jax.numpy as jnp
 from jax import lax
+from jax.experimental import pallas as pl
+from jax.experimental.pallas import tpu as pltpu
 from jax.sharding import PartitionSpec as P
 
 BLOCK = 256
@@ -94,14 +96,65 @@
     )
 
 
-def gathered_rows(pieces):
-    widths = [p.shape[1] for p in pieces]
-    full = lax.all_gather(jnp.concatenate(pieces, axis=1), ("row", "col"), axis=0, tiled=True)
-    out, at = [], 0
-    for w in widths:
-        out.append(full[:, at : at + w])
-        at += w
-    return out
+def leaf_kernel(
+    idx_ref, lower_gate, par_gate, anc_gate, full_hbm, anc_local, pivinv,
+    block_ref, offdiag_ref, par_ref, anc_ref, part_ref,
+    anc_v, lower_v, par_v, ancl_v, rows_v, sem,
+):
+    row, col = idx_ref[0], idx_ref[1]
+    anc_all, order_all = anc_v.shape[0], lower_v.shape[1]
+    width = par_v.shape[1]
+    order_rows, anc_rows = block_ref.shape[0], anc_local.shape[0]
+    off_width = offdiag_ref.shape[1]
+    leaf_at = anc_all + order_all
+    copies = [
+        pltpu.make_async_copy(full_hbm.at[:, pl.ds(0, anc_all)], anc_v, sem.at[0]),
+        pltpu.make_async_copy(full_hbm.at[:, pl.ds(anc_all, order_all)], lower_v, sem.at[1]),
+        pltpu.make_async_copy(
+            full_hbm.at[:, pl.ds(pl.multiple_of(leaf_at + col * width, 128), width)], par_v, sem.at[2]
+        ),
+        pltpu.make_async_copy(
+            full_hbm.at[:, pl.ds(pl.multiple_of(leaf_at + order_all + col * width, 128), width)],
+            ancl_v,
+            sem.at[3],
+        ),
+    ]
+    for copy in copies:
+        copy.start()
+    copies[0].wait()
+    copies[1].wait()
+    lower_v[...] = lower_v[...] * lower_gate[...]
+    lower = lower_v[...]
+    lower_cols = lower_v[:, pl.ds(pl.multiple_of(row * order_rows, 128), order_rows)]
+    offdiag_t = (
+        -jnp.dot(lower_cols.T, anc_v[...], preferred_element_type=jnp.float32)
+    ).astype(jnp.bfloat16)
+    block = pivinv[...] - jnp.dot(offdiag_t, lower, preferred_element_type=jnp.float32)
+    block_ref[...] = block
+    rows = (-jnp.dot(anc_local[...], lower, preferred_element_type=jnp.float32)).astype(jnp.bfloat16)
+    rows_v[...] = rows
+    offdiag_ref[...] = rows_v[:, pl.ds(pl.multiple_of(col * off_width, 128), off_width)]
+    copies[2].wait()
+    copies[3].wait()
+    par_v[...] = par_v[...] * par_gate[...]
+    ancl_v[...] = ancl_v[...] * anc_gate[...]
+    par, ancl = par_v[...], ancl_v[...]
+    upper = jnp.dot(
+        block.astype(jnp.bfloat16), par, preferred_element_type=jnp.float32
+    ) + jnp.dot(offdiag_t, ancl, preferred_element_type=jnp.float32)
+    par_block = (-upper).astype(jnp.bfloat16)
+    lower_sum = jnp.dot(rows, par, preferred_element_type=jnp.float32) + jnp.dot(
+        anc_local[...], ancl, preferred_element_type=jnp.float32
+    )
+    anc_block = (-lower_sum).astype(jnp.bfloat16)
+    par_ref[...] = par_block
+    anc_ref[...] = anc_block
+    par_own = par_v[pl.ds(pl.multiple_of(row * order_rows, 8), order_rows), :]
+    ancl_own = ancl_v[pl.ds(pl.multiple_of(row * anc_rows, 8), anc_rows), :]
+    part = jnp.sum(
+        par_own.astype(jnp.float32) * par_block.astype(jnp.float32), axis=0, keepdims=True
+    ) + jnp.sum(ancl_own.astype(jnp.float32) * anc_block.astype(jnp.float32), axis=0, keepdims=True)
+    part_ref[...] = jnp.broadcast_to(part, part_ref.shape)
 
 
 def local_whole(
@@ -122,57 +175,69 @@
     col_width = leaf_pivots.shape[0]
     off_width = parent_lower.shape[1] // 2
     half = anc_rows // 2
+    anc_all = anc_rows * row_devices
+    order_all = order_rows * row_devices
 
     def mine(x):
         return lax.dynamic_slice_in_dim(x, col_index * half, half, 0)
 
-    anc_full, lower_full, par_full, anc_leaf_full = gathered_rows(
-        [mine(anc_inverse), mine(parent_lower), mine(leaf_lower_par), mine(leaf_lower_anc)]
-    )
-    order_all = order_rows * row_devices
-    parent_gate = jnp.repeat(parent_mask, BLOCK).astype(jnp.bfloat16)
-    leaf_gate = jnp.repeat(leaf_mask, BLOCK).astype(jnp.bfloat16)
-    lower_m = lower_full * parent_gate[:, None]
-    par_m = par_full * leaf_gate[:order_all, None]
-    anc_m = anc_leaf_full * leaf_gate[order_all:, None]
-
-    offdiag_all = (-jnp.dot(anc_full, lower_m, preferred_element_type=jnp.float32)).astype(jnp.bfloat16)
-    lower_cols = lax.dynamic_slice_in_dim(lower_m, row_index * order_rows, order_rows, 1)
-    parent_block = parent_pivinv - lax.dot_general(
-        lower_cols, offdiag_all, (((0,), (0,)), ((), ())), preferred_element_type=jnp.float32
-    )
-    parent_round = parent_block.astype(jnp.bfloat16)
-
-    par_half = lax.dynamic_slice_in_dim(par_m, col_index * col_width, col_width, 1)
-    anc_half = lax.dynamic_slice_in_dim(anc_m, col_index * col_width, col_width, 1)
-    offdiag_cols = lax.dynamic_slice_in_dim(offdiag_all, row_index * order_rows, order_rows, 1)
-    offdiag_rows = lax.dynamic_slice_in_dim(offdiag_all, row_index * anc_rows, anc_rows, 0)
-    upper_sum = jnp.dot(parent_round, par_half, preferred_element_type=jnp.float32) + lax.dot_general(
-        offdiag_cols, anc_half, (((0,), (0,)), ((), ())), preferred_element_type=jnp.float32
-    )
-    lower_sum = jnp.dot(offdiag_rows, par_half, preferred_element_type=jnp.float32) + jnp.dot(
-        anc_inverse, anc_half, preferred_element_type=jnp.float32
-    )
-    leaf_par_block = (-upper_sum).astype(jnp.bfloat16)
-    leaf_anc_block = (-lower_sum).astype(jnp.bfloat16)
-
-    par_own = lax.dynamic_slice_in_dim(par_half, row_index * order_rows, order_rows, 0)
-    anc_own = lax.dynamic_slice_in_dim(anc_half, row_index * anc_rows, anc_rows, 0)
-    partial_sums = jnp.sum(
-        par_own.astype(jnp.float32) * leaf_par_block.astype(jnp.float32), axis=0
-    ) + jnp.sum(anc_own.astype(jnp.float32) * leaf_anc_block.astype(jnp.float32), axis=0)
-    spread = jnp.broadcast_to(partial_sums[None], (row_devices, col_width))
-    column_sums = jnp.sum(lax.all_to_all(spread, "row", 0, 0, tiled=True), axis=0)
+    full = lax.all_gather(
+        jnp.concatenate(
+            [mine(anc_inverse), mine(parent_lower), mine(leaf_lower_par), mine(leaf_lower_anc)], axis=1
+        ),
+        ("row", "col"),
+        axis=0,
+        tiled=True,
+    )
+    parent_gate = jnp.repeat(parent_mask, BLOCK).astype(jnp.bfloat16)[:, None]
+    leaf_gate = jnp.repeat(leaf_mask, BLOCK).astype(jnp.bfloat16)[:, None]
+    idx = jnp.stack([row_index, col_index]).astype(jnp.int32)
+    vmem = pl.BlockSpec(memory_space=pltpu.VMEM)
+    flops = 2 * (3 * order_rows * anc_all * order_all + 4 * order_rows * anc_all * col_width)
+    block, offdiag_own, par_block, anc_block, parts = pl.pallas_call(
+        leaf_kernel,
+        out_shape=(
+            jax.ShapeDtypeStruct((order_rows, order_all), jnp.float32),
+            jax.ShapeDtypeStruct((anc_rows, off_width), jnp.bfloat16),
+            jax.ShapeDtypeStruct((order_rows, col_width), jnp.bfloat16),
+            jax.ShapeDtypeStruct((anc_rows, col_width), jnp.bfloat16),
+            jax.ShapeDtypeStruct((row_devices, col_width), jnp.float32),
+        ),
+        in_specs=[pl.BlockSpec(memory_space=pltpu.SMEM)]
+        + [vmem] * 3
+        + [pl.BlockSpec(memory_space=pl.ANY)]
+        + [vmem] * 2,
+        out_specs=(vmem,) * 5,
+        scratch_shapes=[
+            pltpu.VMEM((anc_all, anc_all), jnp.bfloat16),
+            pltpu.VMEM((anc_all, order_all), jnp.bfloat16),
+            pltpu.VMEM((order_all, col_width), jnp.bfloat16),
+            pltpu.VMEM((anc_all, col_width), jnp.bfloat16),
+            pltpu.VMEM((anc_rows, order_all), jnp.bfloat16),
+            pltpu.SemaphoreType.DMA((4,)),
+        ],
+        cost_estimate=pl.CostEstimate(
+            flops=flops, transcendentals=0, bytes_accessed=full.size + 8 * anc_rows * order_all
+        ),
+    )(
+        idx,
+        parent_gate,
+        leaf_gate[:order_all],
+        leaf_gate[order_all:],
+        full,
+        anc_inverse,
+        parent_pivinv,
+    )
+    column_sums = jnp.sum(lax.all_to_all(parts, "row", 0, 0, tiled=True), axis=0)
     density = leaf_pivots - column_sums
-    offdiag_own = lax.dynamic_slice_in_dim(offdiag_rows, col_index * off_width, off_width, 1)
-    return parent_block, offdiag_own, leaf_par_block, leaf_anc_block, density
+    return block, offdiag_own, par_block, anc_block, density
 
 
 def fits_whole(mesh, anc_rows, order_rows):
     anc_all = anc_rows * mesh.shape["row"]
     return (
         anc_rows == order_rows
-        and anc_rows % 2 == 0
+        and anc_rows % 128 == 0
         and anc_all * anc_all * 2 <= 16 * 1024 * 1024
     )
 

time: 117 us -> 113 us (0.966)
  waiting for transfers between devices: 83.8 us -> 73.4 us
  blocking collectives: 0 us -> 9.28 us
  matrix products: 7.24 us -> 0 us
  Pallas kernels: 0 us -> 6.44 us
  starting transfers between devices: 3.34 us -> 0.04 us
  local copies, waits for them, and re-layouts: 3.73 us -> 5.66 us
  other arithmetic: 4.7 us -> 3.41 us
    all_to_all x0 -> x1, blocking collectives: none -> 9.28 us  [local_whole(): lax.all_to_all(parts, 'row', 0, 0, tiled=True)]
    dot_general x6 -> x0, matrix products: 7.24 us -> none  [the longest x1 4.01 us: local_whole(): jnp.dot(anc_full, lower_m, preferred_element_type=jnp.float32)]
    pallas_call x0 -> x1, Pallas kernels: none -> 6.44 us  [local_whole(): pl.pallas_call(leaf_kernel, out_shape=(jax.ShapeDtypeStruct((order_rows,...]
    all_to_all x1 -> x0, waiting for transfers between devices: 5.73 us -> none  [local_whole(): lax.all_to_all(spread, 'row', 0, 0, tiled=True)]
    all_gather x1, waiting for transfers between devices: 78 us -> 73.4 us  [local_whole(): lax.all_gather(jnp.concatenate([mine(anc_inverse), mine(parent_lower), mi...]
    all_to_all x1 -> x0, starting transfers between devices: 3.31 us -> none  [local_whole(): lax.all_to_all(spread, 'row', 0, 0, tiled=True)]
    mul x1 -> x0, other arithmetic: 3.24 us -> none  [local_whole(): anc_m = anc_leaf_full * leaf_gate[order_all:, None]]
    unnamed x17 -> x10, local copies, waits for them, and re-layouts: 0.28 us -> 2.87 us
  transfers between devices with their start and end apart: 2 -> 1, of which waited for: 2 -> 1; matrix products, arithmetic and copies ran while one was open for 1% -> 4% of each run, Pallas kernels for 0% -> 0%
where the time goes in v4:
time: 113 us; the launch traced here: 112 us
  waiting for transfers between devices  73.4 us (65%)
  between operations  14.1 us (12%)
  blocking collectives  9.28 us (8%)
  Pallas kernels  6.44 us (6%)
  local copies, waits for them, and re-layouts  5.66 us (5%)
  other arithmetic  3.41 us (3%)
    all_gather x1, waiting for transfers between devices, local_whole(): lax.all_gather(jnp.concatenate([mine(anc_inverse), mine(parent_lower), mi...  73.4 us
    all_to_all x1, blocking collectives, local_whole(): lax.all_to_all(parts, 'row', 0, 0, tiled=True)  9.28 us
    pallas_call x1, Pallas kernels, local_whole(): pl.pallas_call(leaf_kernel, out_shape=(jax.ShapeDtypeStruct((order_rows,...  6.44 us
    unnamed x10, local copies, waits for them, and re-layouts  2.87 us
  transfers between devices with their start and end apart: 1, of which 1 were waited for; matrix products, arithmetic and copies ran while one was open for 4% of the time, Pallas kernels for 0%

profile of v4, /device:TPU:0, one launch (start us, length us, event | category | flops | bytes accessed | tf_op | source)
XLA Modules:
  0.0 112.3 jit_solution(467864254485588343)
XLA Ops:
  7.2 0.0 copy-start
  7.2 0.0 all-gather.2.cloned.1.call-start
  7.2 1.0 constant_dynamic-slice_fusion.2
  8.2 1.0 constant_dynamic-slice_fusion
  9.2 0.8 pad_maximum_fusion
  10.0 0.0 all-gather.2.cloned.1.call-update
  10.1 0.7 convert_element_type.19
  10.7 0.7 convert_element_type.21
  11.4 0.1 broadcast_bitcast_fusion.2
  11.5 0.1 fusion
  11.6 0.1 broadcast_bitcast_fusion
  11.6 0.9 copy.23
  12.5 0.9 copy.25
  13.4 0.9 copy.21
  14.3 0.7 pad_add_fusion.idx_ref
  15.0 73.4 %all-gather.2.cloned.1.call-done.full_hbm = bf16[1024,4096]{1,0:T(8,128)(2,1)} async-done(((bf16[64,4096]{1,0:T(8,128)(2,1)}), bf16[1024,4096]{1,0:T(8,128)(2,1)}) %all-gather.2.cloned.1.call-update) | async-done | bytes 8388624 | tf_op jit(solution)/shard_map/all_gather | solution.py:184
  88.4 6.4 %shard_map.119 = (f32[128,1024]{1,0:T(8,128)}, bf16[128,512]{1,0:T(8,128)(2,1)}, bf16[128,512]{1,0:T(8,128)(2,1)}, bf16[128,512]{1,0:T(8,128)(2,1)}, f32[8,512]{1,0:T(8,128)}) custom-call(s32[2]{0:T(128)} %pad_add_fusion.idx_ref, bf16[1024,1]{1,0:T(8,128)(2,1)} %bitcast.20, bf16[1024,1]{1,0:T(8,128)(2,1)} %bitcast.18, bf16[1024,1]{1,0:T(8,128)(2,1)} %bitcast.19, ...), custom_call_target="tpu_custom_call" | custom-call | flops 1342177280 | bytes 5242880 | tf_op jit(solution)/shard_map/pallas_call | solution.py:197
  94.8 0.7 copy.19
  95.6 9.3 %all_to_all.9 = f32[8,1,512]{2,1,0:T(1,128)S(1)} all-to-all(f32[8,1,512]{2,1,0:T(1,128)S(1)} %copy.19), channel_id=1, replica_groups=mesh['pole'=2,'row'=8,'col'=2] {'row'}, dimensions={0} | all-to-all | bytes 32768 | tf_op jit(solution)/shard_map/all_to_all | solution.py:231
  104.9 0.0 copy-done
  104.9 0.6 sub.3
  (4 shorter events, 0.0 us)
Async XLA Ops:
  7.2 97.7 %copy-start = (f32[512]{0:T(512)S(1)}, f32[512]{0:T(512)}, u32[]{:S(2)}) copy-start(f32[512]{0:T(512)} %param.15) | copy-start | bytes 6148
  7.2 81.2 %all-gather.2.cloned.1.call-start = ((), (), s32[]{:S(2)}) async-start(), calls=%async_computation.1 | async-start | bytes 8912896 | tf_op jit(solution)/shard_map/all_gather | solution.py:184
Sparse Core Ops, SparseCore 0:
  10.7 77.5 all-gather.1

commit v5 on v4

--- a/solution.py
+++ b/solution.py
@@ -96,25 +96,57 @@
     )
 
 
+def piece_kernel(idx_ref, anc_hbm, lower_hbm, par_hbm, ancl_hbm, out_ref, sem):
+    row, col = idx_ref[0], idx_ref[1]
+    half = out_ref.shape[0]
+    blk = anc_hbm.shape[0]
+    blocks = anc_hbm.shape[1] // blk
+    sent = blocks // 2 + 1
+    rows = pl.ds(pl.multiple_of(col * half, 8), half)
+    copies = []
+    for k in range(sent):
+        start = pl.multiple_of(lax.rem(row + k, blocks) * blk, 128)
+        copies.append(
+            pltpu.make_async_copy(
+                anc_hbm.at[rows, pl.ds(start, blk)], out_ref.at[:, pl.ds(k * blk, blk)], sem.at[k]
+            )
+        )
+    at = sent * blk
+    for j, source in enumerate((lower_hbm, par_hbm, ancl_hbm)):
+        width = source.shape[1]
+        copies.append(
+            pltpu.make_async_copy(
+                source.at[rows, :], out_ref.at[:, pl.ds(at, width)], sem.at[sent + j]
+            )
+        )
+        at += width
+    for copy in copies:
+        copy.start()
+    for copy in copies:
+        copy.wait()
+
+
 def leaf_kernel(
     idx_ref, lower_gate, par_gate, anc_gate, full_hbm, anc_local, pivinv,
     block_ref, offdiag_ref, par_ref, anc_ref, part_ref,
-    anc_v, lower_v, par_v, ancl_v, rows_v, sem,
+    sent_v, anc_v, lower_v, par_v, ancl_v, rows_v, sem,
 ):
     row, col = idx_ref[0], idx_ref[1]
     anc_all, order_all = anc_v.shape[0], lower_v.shape[1]
     width = par_v.shape[1]
     order_rows, anc_rows = block_ref.shape[0], anc_local.shape[0]
     off_width = offdiag_ref.shape[1]
-    leaf_at = anc_all + order_all
+    sent_width = sent_v.shape[1]
+    leaf_at = sent_width + order_all
+    leaf_width = (full_hbm.shape[1] - leaf_at) // 2
     copies = [
-        pltpu.make_async_copy(full_hbm.at[:, pl.ds(0, anc_all)], anc_v, sem.at[0]),
-        pltpu.make_async_copy(full_hbm.at[:, pl.ds(anc_all, order_all)], lower_v, sem.at[1]),
+        pltpu.make_async_copy(full_hbm.at[:, pl.ds(0, sent_width)], sent_v, sem.at[0]),
+        pltpu.make_async_copy(full_hbm.at[:, pl.ds(sent_width, order_all)], lower_v, sem.at[1]),
         pltpu.make_async_copy(
             full_hbm.at[:, pl.ds(pl.multiple_of(leaf_at + col * width, 128), width)], par_v, sem.at[2]
         ),
         pltpu.make_async_copy(
-            full_hbm.at[:, pl.ds(pl.multiple_of(leaf_at + order_all + col * width, 128), width)],
+            full_hbm.at[:, pl.ds(pl.multiple_of(leaf_at + leaf_width + col * width, 128), width)],
             ancl_v,
             sem.at[3],
         ),
@@ -122,6 +154,17 @@
     for copy in copies:
         copy.start()
     copies[0].wait()
+    blocks = anc_all // anc_rows
+    for p in range(blocks):
+        for q in range(blocks):
+            k = (q - p) % blocks
+            if k * anc_rows < sent_width:
+                part = sent_v[p * anc_rows : (p + 1) * anc_rows, k * anc_rows : (k + 1) * anc_rows]
+            else:
+                k = (p - q) % blocks
+                part = sent_v[q * anc_rows : (q + 1) * anc_rows, k * anc_rows : (k + 1) * anc_rows]
+                part = part.astype(jnp.float32).T.astype(jnp.bfloat16)
+            anc_v[p * anc_rows : (p + 1) * anc_rows, q * anc_rows : (q + 1) * anc_rows] = part
     copies[1].wait()
     lower_v[...] = lower_v[...] * lower_gate[...]
     lower = lower_v[...]
@@ -178,20 +221,20 @@
     anc_all = anc_rows * row_devices
     order_all = order_rows * row_devices
 
-    def mine(x):
-        return lax.dynamic_slice_in_dim(x, col_index * half, half, 0)
-
-    full = lax.all_gather(
-        jnp.concatenate(
-            [mine(anc_inverse), mine(parent_lower), mine(leaf_lower_par), mine(leaf_lower_anc)], axis=1
-        ),
-        ("row", "col"),
-        axis=0,
-        tiled=True,
-    )
+    idx = jnp.stack([row_index, col_index]).astype(jnp.int32)
+    sent_width = (row_devices // 2 + 1) * anc_rows
+    piece_width = sent_width + order_all + 2 * leaf_lower_par.shape[1]
+    hbm = pl.BlockSpec(memory_space=pl.ANY)
+    piece = pl.pallas_call(
+        piece_kernel,
+        out_shape=jax.ShapeDtypeStruct((half, piece_width), jnp.bfloat16),
+        in_specs=[pl.BlockSpec(memory_space=pltpu.SMEM)] + [hbm] * 4,
+        out_specs=pl.BlockSpec(memory_space=pltpu.VMEM),
+        scratch_shapes=[pltpu.SemaphoreType.DMA((row_devices // 2 + 4,))],
+    )(idx, anc_inverse, parent_lower, leaf_lower_par, leaf_lower_anc)
+    full = lax.all_gather(piece, ("row", "col"), axis=0, tiled=True)
     parent_gate = jnp.repeat(parent_mask, BLOCK).astype(jnp.bfloat16)[:, None]
     leaf_gate = jnp.repeat(leaf_mask, BLOCK).astype(jnp.bfloat16)[:, None]
-    idx = jnp.stack([row_index, col_index]).astype(jnp.int32)
     vmem = pl.BlockSpec(memory_space=pltpu.VMEM)
     flops = 2 * (3 * order_rows * anc_all * order_all + 4 * order_rows * anc_all * col_width)
     block, offdiag_own, par_block, anc_block, parts = pl.pallas_call(
@@ -209,6 +252,7 @@
         + [vmem] * 2,
         out_specs=(vmem,) * 5,
         scratch_shapes=[
+            pltpu.VMEM((anc_all, sent_width), jnp.bfloat16),
             pltpu.VMEM((anc_all, anc_all), jnp.bfloat16),
             pltpu.VMEM((anc_all, order_all), jnp.bfloat16),
             pltpu.VMEM((order_all, col_width), jnp.bfloat16),

time: 113 us -> 108 us (0.956)
  waiting for transfers between devices: 73.4 us -> 68.8 us
  Pallas kernels: 6.44 us -> 8.83 us
  local copies, waits for them, and re-layouts: 5.66 us -> 3.66 us
    all_gather x1, waiting for transfers between devices: 73.4 us -> 68.8 us  [local_whole(): full = lax.all_gather(piece, ('row', 'col'), axis=0, tiled=True)]
    pallas_call x0 -> x1, Pallas kernels: none -> 2.63 us  [local_whole(): pl.pallas_call(piece_kernel, out_shape=jax.ShapeDtypeStruct((half, piece_...]
    dynamic_slice x2 -> x0, local copies, waits for them, and re-layouts: 1.98 us -> none  [mine(): return lax.dynamic_slice_in_dim(x, col_index * half, half, 0)]
where the time goes in v5:
time: 108 us; the launch traced here: 107 us
  waiting for transfers between devices  68.8 us (64%)
  between operations  14.1 us (13%)
  blocking collectives  9.41 us (9%)
  Pallas kernels  8.83 us (8%)
  local copies, waits for them, and re-layouts  3.66 us (3%)
  other arithmetic  2.57 us (2%)
    all_gather x1, waiting for transfers between devices, local_whole(): full = lax.all_gather(piece, ('row', 'col'), axis=0, tiled=True)  68.8 us
    all_to_all x1, blocking collectives, local_whole(): lax.all_to_all(parts, 'row', 0, 0, tiled=True)  9.41 us
    pallas_call x1, Pallas kernels, local_whole(): pl.pallas_call(leaf_kernel, out_shape=(jax.ShapeDtypeStruct((order_rows,...  6.2 us
    unnamed x10, local copies, waits for them, and re-layouts  2.85 us
    pallas_call x1, Pallas kernels, local_whole(): pl.pallas_call(piece_kernel, out_shape=jax.ShapeDtypeStruct((half, piece_...  2.63 us
  transfers between devices with their start and end apart: 1, of which 1 were waited for; matrix products, arithmetic and copies ran while one was open for 4% of the time, Pallas kernels for 0%

profile of v5, /device:TPU:0, one launch (start us, length us, event | category | flops | bytes accessed | tf_op | source)
XLA Modules:
  0.0 107.4 jit_solution(3486012663531449335)
XLA Ops:
  7.2 0.0 copy-start
  7.2 0.0 all-gather.2.cloned.1.call-start
  7.2 0.6 pad_add_fusion.idx_ref
  7.9 2.6 %shard_map.119 = bf16[64,3712]{1,0:T(8,128)(2,1)} custom-call(s32[2]{0:T(128)} %pad_add_fusion.idx_ref, bf16[128,1024]{1,0:T(8,128)(2,1)} %anc_local.1, bf16[128,1024]{1,0:T(8,128)(2,1)} %lower_hbm.1, bf16[128,1024]{1,0:T(8,128)(2,1)} %par_hbm.1, bf16[128,1024]{1,0:T(8,128)(2,1)} %ancl_hbm.1), custom_call_target="tpu_custom_call" | custom-call | tf_op jit(solution)/shard_map/pallas_call | solution.py:228
  10.5 0.0 all-gather.2.cloned.1.call-update
  10.5 0.7 convert_element_type.19
  11.2 0.7 convert_element_type.21
  11.8 0.1 broadcast_bitcast_fusion.2
  11.9 0.1 fusion
  12.0 0.1 broadcast_bitcast_fusion
  12.1 0.9 copy.23
  13.0 0.9 copy.25
  13.9 0.9 copy.21
  14.8 68.8 %all-gather.2.cloned.1.call-done.full_hbm = bf16[1024,3712]{1,0:T(8,128)(2,1)} async-done(((bf16[64,3712]{1,0:T(8,128)(2,1)}), bf16[1024,3712]{1,0:T(8,128)(2,1)}) %all-gather.2.cloned.1.call-update) | async-done | bytes 7602192 | tf_op jit(solution)/shard_map/all_gather | solution.py:235
  83.5 6.2 %shard_map.120 = (f32[128,1024]{1,0:T(8,128)}, bf16[128,512]{1,0:T(8,128)(2,1)}, bf16[128,512]{1,0:T(8,128)(2,1)}, bf16[128,512]{1,0:T(8,128)(2,1)}, f32[8,512]{1,0:T(8,128)}) custom-call(s32[2]{0:T(128)} %pad_add_fusion.idx_ref, bf16[1024,1]{1,0:T(8,128)(2,1)} %bitcast.20, bf16[1024,1]{1,0:T(8,128)(2,1)} %bitcast.18, bf16[1024,1]{1,0:T(8,128)(2,1)} %bitcast.19, ...), custom_call_target="tpu_custom_call" | custom-call | flops 1342177280 | bytes 4849664 | tf_op jit(solution)/shard_map/pallas_call | solution.py:240
  89.7 0.7 copy.19
  90.5 9.4 %all_to_all.9 = f32[8,1,512]{2,1,0:T(1,128)S(1)} all-to-all(f32[8,1,512]{2,1,0:T(1,128)S(1)} %copy.19), channel_id=1, replica_groups=mesh['pole'=2,'row'=8,'col'=2] {'row'}, dimensions={0} | all-to-all | bytes 32768 | tf_op jit(solution)/shard_map/all_to_all | solution.py:275
  99.9 0.0 copy-done
  99.9 0.6 sub.3
  (4 shorter events, 0.0 us)
Async XLA Ops:
  7.2 92.8 %copy-start = (f32[512]{0:T(512)S(1)}, f32[512]{0:T(512)}, u32[]{:S(2)}) copy-start(f32[512]{0:T(512)} %param.15) | copy-start | bytes 6148
  7.2 76.4 %all-gather.2.cloned.1.call-start = ((), (), s32[]{:S(2)}) async-start(), calls=%async_computation.1 | async-start | bytes 8077312 | tf_op jit(solution)/shard_map/all_gather | solution.py:235
Sparse Core Ops, SparseCore 0:
  10.9 72.6 all-gather.1

commit v6 on v5

--- a/solution.py
+++ b/solution.py
@@ -96,42 +96,29 @@
     )
 
 
-def piece_kernel(idx_ref, anc_hbm, lower_hbm, par_hbm, ancl_hbm, out_ref, sem):
-    row, col = idx_ref[0], idx_ref[1]
+def piece_kernel(anc_hbm, lower_hbm, par_hbm, ancl_hbm, out_ref):
+    row, col = lax.axis_index("row"), lax.axis_index("col")
     half = out_ref.shape[0]
     blk = anc_hbm.shape[0]
     blocks = anc_hbm.shape[1] // blk
     sent = blocks // 2 + 1
     rows = pl.ds(pl.multiple_of(col * half, 8), half)
-    copies = []
     for k in range(sent):
         start = pl.multiple_of(lax.rem(row + k, blocks) * blk, 128)
-        copies.append(
-            pltpu.make_async_copy(
-                anc_hbm.at[rows, pl.ds(start, blk)], out_ref.at[:, pl.ds(k * blk, blk)], sem.at[k]
-            )
-        )
+        out_ref[:, k * blk : (k + 1) * blk] = anc_hbm[rows, pl.ds(start, blk)]
     at = sent * blk
-    for j, source in enumerate((lower_hbm, par_hbm, ancl_hbm)):
+    for source in (lower_hbm, par_hbm, ancl_hbm):
         width = source.shape[1]
-        copies.append(
-            pltpu.make_async_copy(
-                source.at[rows, :], out_ref.at[:, pl.ds(at, width)], sem.at[sent + j]
-            )
-        )
+        out_ref[:, at : at + width] = source[rows, :]
         at += width
-    for copy in copies:
-        copy.start()
-    for copy in copies:
-        copy.wait()
 
 
 def leaf_kernel(
-    idx_ref, lower_gate, par_gate, anc_gate, full_hbm, anc_local, pivinv,
+    lower_gate, par_gate, anc_gate, pivots, full_hbm, anc_local, pivinv,
     block_ref, offdiag_ref, par_ref, anc_ref, part_ref,
     sent_v, anc_v, lower_v, par_v, ancl_v, rows_v, sem,
 ):
-    row, col = idx_ref[0], idx_ref[1]
+    row, col = lax.axis_index("row"), lax.axis_index("col")
     anc_all, order_all = anc_v.shape[0], lower_v.shape[1]
     width = par_v.shape[1]
     order_rows, anc_rows = block_ref.shape[0], anc_local.shape[0]
@@ -197,6 +184,7 @@
     part = jnp.sum(
         par_own.astype(jnp.float32) * par_block.astype(jnp.float32), axis=0, keepdims=True
     ) + jnp.sum(ancl_own.astype(jnp.float32) * anc_block.astype(jnp.float32), axis=0, keepdims=True)
+    part = jnp.where(row == 0, pivots[...] - part, -part)
     part_ref[...] = jnp.broadcast_to(part, part_ref.shape)
 
 
@@ -221,17 +209,14 @@
     anc_all = anc_rows * row_devices
     order_all = order_rows * row_devices
 
-    idx = jnp.stack([row_index, col_index]).astype(jnp.int32)
     sent_width = (row_devices // 2 + 1) * anc_rows
     piece_width = sent_width + order_all + 2 * leaf_lower_par.shape[1]
-    hbm = pl.BlockSpec(memory_space=pl.ANY)
     piece = pl.pallas_call(
         piece_kernel,
         out_shape=jax.ShapeDtypeStruct((half, piece_width), jnp.bfloat16),
-        in_specs=[pl.BlockSpec(memory_space=pltpu.SMEM)] + [hbm] * 4,
+        in_specs=[pl.BlockSpec(memory_space=pltpu.VMEM)] * 4,
         out_specs=pl.BlockSpec(memory_space=pltpu.VMEM),
-        scratch_shapes=[pltpu.SemaphoreType.DMA((row_devices // 2 + 4,))],
-    )(idx, anc_inverse, parent_lower, leaf_lower_par, leaf_lower_anc)
+    )(anc_inverse, parent_lower, leaf_lower_par, leaf_lower_anc)
     full = lax.all_gather(piece, ("row", "col"), axis=0, tiled=True)
     parent_gate = jnp.repeat(parent_mask, BLOCK).astype(jnp.bfloat16)[:, None]
     leaf_gate = jnp.repeat(leaf_mask, BLOCK).astype(jnp.bfloat16)[:, None]
@@ -246,8 +231,7 @@
             jax.ShapeDtypeStruct((anc_rows, col_width), jnp.bfloat16),
             jax.ShapeDtypeStruct((row_devices, col_width), jnp.float32),
         ),
-        in_specs=[pl.BlockSpec(memory_space=pltpu.SMEM)]
-        + [vmem] * 3
+        in_specs=[vmem] * 4
         + [pl.BlockSpec(memory_space=pl.ANY)]
         + [vmem] * 2,
         out_specs=(vmem,) * 5,
@@ -264,16 +248,15 @@
             flops=flops, transcendentals=0, bytes_accessed=full.size + 8 * anc_rows * order_all
         ),
     )(
-        idx,
         parent_gate,
         leaf_gate[:order_all],
         leaf_gate[order_all:],
+        leaf_pivots[None, :],
         full,
         anc_inverse,
         parent_pivinv,
     )
-    column_sums = jnp.sum(lax.all_to_all(parts, "row", 0, 0, tiled=True), axis=0)
-    density = leaf_pivots - column_sums
+    density = jnp.sum(lax.all_to_all(parts, "row", 0, 0), axis=0)
     return block, offdiag_own, par_block, anc_block, density
 
 

time: 108 us -> 108 us (level)
  waiting for transfers between devices: 68.8 us -> 70 us
    all_gather x1, waiting for transfers between devices: 68.8 us -> 70 us  [local_whole(): full = lax.all_gather(piece, ('row', 'col'), axis=0, tiled=True)]
    unnamed x10 -> x8, local copies, waits for them, and re-layouts: 2.85 us -> 2.85 us
where the time goes in v6:
time: 108 us; the launch traced here: 107 us
  waiting for transfers between devices  70 us (65%)
  between operations  14 us (13%)
  blocking collectives  9.4 us (9%)
  Pallas kernels  8.26 us (8%)
  local copies, waits for them, and re-layouts  3.66 us (3%)
  other arithmetic  1.92 us (2%)
    all_gather x1, waiting for transfers between devices, local_whole(): full = lax.all_gather(piece, ('row', 'col'), axis=0, tiled=True)  70 us
    all_to_all x1, blocking collectives, local_whole(): density = jnp.sum(lax.all_to_all(parts, 'row', 0, 0), axis=0)  9.4 us
    pallas_call x1, Pallas kernels, local_whole(): pl.pallas_call(leaf_kernel, out_shape=(jax.ShapeDtypeStruct((order_rows,...  6.25 us
    unnamed x8, local copies, waits for them, and re-layouts  2.85 us
  transfers between devices with their start and end apart: 1, of which 1 were waited for; matrix products, arithmetic and copies ran while one was open for 4% of the time, Pallas kernels for 0%

profile of v6, /device:TPU:0, one launch (start us, length us, event | category | flops | bytes accessed | tf_op | source)
XLA Modules:
  0.0 107.4 jit_solution(16338553378267592968)
XLA Ops:
  7.2 0.0 all-gather.2.cloned.1.call-start
  7.2 2.0 %shard_map.119 = bf16[64,3712]{1,0:T(8,128)(2,1)} custom-call(bf16[128,1024]{1,0:T(8,128)(2,1)} %anc_local.1, bf16[128,1024]{1,0:T(8,128)(2,1)} %lower_hbm.1, bf16[128,1024]{1,0:T(8,128)(2,1)} %par_hbm.1, bf16[128,1024]{1,0:T(8,128)(2,1)} %ancl_hbm.1), custom_call_target="tpu_custom_call" | custom-call | tf_op jit(solution)/shard_map/pallas_call | solution.py:214
  9.2 0.0 all-gather.2.cloned.1.call-update
  9.2 0.7 convert_element_type.19
  9.9 0.7 convert_element_type.21
  10.6 0.1 broadcast_bitcast_fusion.2
  10.6 0.1 fusion
  10.7 0.1 broadcast_bitcast_fusion
  10.8 0.9 copy.23
  11.7 0.9 copy.25
  12.6 0.9 copy.21
  13.5 70.0 %all-gather.2.cloned.1.call-done.full_hbm = bf16[1024,3712]{1,0:T(8,128)(2,1)} async-done(((bf16[64,3712]{1,0:T(8,128)(2,1)}), bf16[1024,3712]{1,0:T(8,128)(2,1)}) %all-gather.2.cloned.1.call-update) | async-done | bytes 7602192 | tf_op jit(solution)/shard_map/all_gather | solution.py:220
  83.5 6.3 %shard_map.120 = (f32[128,1024]{1,0:T(8,128)}, bf16[128,512]{1,0:T(8,128)(2,1)}, bf16[128,512]{1,0:T(8,128)(2,1)}, bf16[128,512]{1,0:T(8,128)(2,1)}, f32[8,512]{1,0:T(8,128)}) custom-call(bf16[1024,1]{1,0:T(8,128)(2,1)} %bitcast.19, bf16[1024,1]{1,0:T(8,128)(2,1)} %bitcast.17, bf16[1024,1]{1,0:T(8,128)(2,1)} %bitcast.18, f32[1,512]{1,0:T(1,128)} %bitcast.24, ...), custom_call_target="tpu_custom_call" | custom-call | flops 1342177280 | bytes 4849664 | tf_op jit(solution)/shard_map/pallas_call | solution.py:225
  89.8 0.7 copy.19
  90.5 9.4 %all_to_all.9 = f32[8,1,512]{2,1,0:T(1,128)S(1)} all-to-all(f32[8,1,512]{2,1,0:T(1,128)S(1)} %copy.19), channel_id=1, replica_groups=mesh['pole'=2,'row'=8,'col'=2] {'row'}, dimensions={0} | all-to-all | bytes 32768 | tf_op jit(solution)/shard_map/all_to_all | solution.py:259
  99.9 0.6 reduce_sum.9
  (3 shorter events, 0.0 us)
Async XLA Ops:
  7.2 76.4 %all-gather.2.cloned.1.call-start = ((), (), s32[]{:S(2)}) async-start(), calls=%async_computation.1 | async-start | bytes 8077312 | tf_op jit(solution)/shard_map/all_gather | solution.py:220
Sparse Core Ops, SparseCore 0:
  10.9 72.6 all-gather.1

commit v7 on v6

--- a/solution.py
+++ b/solution.py
@@ -153,34 +153,42 @@
                 part = part.astype(jnp.float32).T.astype(jnp.bfloat16)
             anc_v[p * anc_rows : (p + 1) * anc_rows, q * anc_rows : (q + 1) * anc_rows] = part
     copies[1].wait()
-    lower_v[...] = lower_v[...] * lower_gate[...]
     lower = lower_v[...]
-    lower_cols = lower_v[:, pl.ds(pl.multiple_of(row * order_rows, 128), order_rows)]
+    gate_row = lower_gate[...]
+    lower_cols = lower_v[:, pl.ds(pl.multiple_of(row * order_rows, 128), order_rows)] * gate_row
     offdiag_t = (
         -jnp.dot(lower_cols.T, anc_v[...], preferred_element_type=jnp.float32)
     ).astype(jnp.bfloat16)
-    block = pivinv[...] - jnp.dot(offdiag_t, lower, preferred_element_type=jnp.float32)
+    gate_col = gate_row.T
+    block = pivinv[...] - jnp.dot(offdiag_t * gate_col, lower, preferred_element_type=jnp.float32)
     block_ref[...] = block
-    rows = (-jnp.dot(anc_local[...], lower, preferred_element_type=jnp.float32)).astype(jnp.bfloat16)
+    anc_here = anc_local[...]
+    rows = (-jnp.dot(anc_here * gate_col, lower, preferred_element_type=jnp.float32)).astype(
+        jnp.bfloat16
+    )
     rows_v[...] = rows
     offdiag_ref[...] = rows_v[:, pl.ds(pl.multiple_of(col * off_width, 128), off_width)]
     copies[2].wait()
     copies[3].wait()
-    par_v[...] = par_v[...] * par_gate[...]
-    ancl_v[...] = ancl_v[...] * anc_gate[...]
+    par_col = par_gate[...].T
+    anc_col = anc_gate[...].T
     par, ancl = par_v[...], ancl_v[...]
     upper = jnp.dot(
-        block.astype(jnp.bfloat16), par, preferred_element_type=jnp.float32
-    ) + jnp.dot(offdiag_t, ancl, preferred_element_type=jnp.float32)
+        block.astype(jnp.bfloat16) * par_col, par, preferred_element_type=jnp.float32
+    ) + jnp.dot(offdiag_t * anc_col, ancl, preferred_element_type=jnp.float32)
     par_block = (-upper).astype(jnp.bfloat16)
-    lower_sum = jnp.dot(rows, par, preferred_element_type=jnp.float32) + jnp.dot(
-        anc_local[...], ancl, preferred_element_type=jnp.float32
+    lower_sum = jnp.dot(rows * par_col, par, preferred_element_type=jnp.float32) + jnp.dot(
+        anc_here * anc_col, ancl, preferred_element_type=jnp.float32
     )
     anc_block = (-lower_sum).astype(jnp.bfloat16)
     par_ref[...] = par_block
     anc_ref[...] = anc_block
-    par_own = par_v[pl.ds(pl.multiple_of(row * order_rows, 8), order_rows), :]
-    ancl_own = ancl_v[pl.ds(pl.multiple_of(row * anc_rows, 8), anc_rows), :]
+    par_own = par_v[pl.ds(pl.multiple_of(row * order_rows, 8), order_rows), :] * par_gate[
+        pl.ds(pl.multiple_of(row * order_rows, 8), order_rows), :
+    ]
+    ancl_own = ancl_v[pl.ds(pl.multiple_of(row * anc_rows, 8), anc_rows), :] * anc_gate[
+        pl.ds(pl.multiple_of(row * anc_rows, 8), anc_rows), :
+    ]
     part = jnp.sum(
         par_own.astype(jnp.float32) * par_block.astype(jnp.float32), axis=0, keepdims=True
     ) + jnp.sum(ancl_own.astype(jnp.float32) * anc_block.astype(jnp.float32), axis=0, keepdims=True)
@@ -229,7 +237,7 @@
             jax.ShapeDtypeStruct((anc_rows, off_width), jnp.bfloat16),
             jax.ShapeDtypeStruct((order_rows, col_width), jnp.bfloat16),
             jax.ShapeDtypeStruct((anc_rows, col_width), jnp.bfloat16),
-            jax.ShapeDtypeStruct((row_devices, col_width), jnp.float32),
+            jax.ShapeDtypeStruct((1, col_width), jnp.float32),
         ),
         in_specs=[vmem] * 4
         + [pl.BlockSpec(memory_space=pl.ANY)]
@@ -256,7 +264,12 @@
         anc_inverse,
         parent_pivinv,
     )
-    density = jnp.sum(lax.all_to_all(parts, "row", 0, 0), axis=0)
+    step = 1
+    while step < row_devices:
+        pairs = [(i, i ^ step) for i in range(row_devices)]
+        parts = parts + lax.ppermute(parts, "row", pairs)
+        step *= 2
+    density = parts[0]
     return block, offdiag_own, par_block, anc_block, density
 
 
@@ -265,6 +278,7 @@
     return (
         anc_rows == order_rows
         and anc_rows % 128 == 0
+        and mesh.shape["row"] & (mesh.shape["row"] - 1) == 0
         and anc_all * anc_all * 2 <= 16 * 1024 * 1024
     )
 

time: 108 us -> 110 us (1.019)
  blocking collectives: 9.4 us -> 0 us
  waiting for transfers between devices: 70 us -> 78.5 us
  starting transfers between devices: 0.04 us -> 3.55 us
    all_to_all x1 -> x0, blocking collectives: 9.4 us -> none  [local_whole(): density = jnp.sum(lax.all_to_all(parts, 'row', 0, 0), axis=0)]
    ppermute x0 -> x3, waiting for transfers between devices: none -> 8.42 us  [local_whole(): parts = parts + lax.ppermute(parts, 'row', pairs)]
    ppermute x0 -> x3, starting transfers between devices: none -> 3.51 us  [local_whole(): parts = parts + lax.ppermute(parts, 'row', pairs)]
    add x0 -> x3, other arithmetic: none -> 1.27 us  [local_whole(): parts = parts + lax.ppermute(parts, 'row', pairs)]
  transfers between devices with their start and end apart: 1 -> 4, of which waited for: 1 -> 4; matrix products, arithmetic and copies ran while one was open for 4% -> 4% of each run, Pallas kernels for 0% -> 0%
where the time goes in v7:
time: 110 us
  waiting for transfers between devices  78.5 us (71%)
  between operations  14 us (13%)
  Pallas kernels  8.24 us (7%)
  starting transfers between devices  3.55 us (3%)
  local copies, waits for them, and re-layouts  2.93 us (3%)
  other arithmetic  2.59 us (2%)
    all_gather x1, waiting for transfers between devices, local_whole(): full = lax.all_gather(piece, ('row', 'col'), axis=0, tiled=True)  70 us
    ppermute x3, waiting for transfers between devices, local_whole(): parts = parts + lax.ppermute(parts, 'row', pairs)  8.42 us
    pallas_call x1, Pallas kernels, local_whole(): pl.pallas_call(leaf_kernel, out_shape=(jax.ShapeDtypeStruct((order_rows,...  6.24 us
    ppermute x3, starting transfers between devices, local_whole(): parts = parts + lax.ppermute(parts, 'row', pairs)  3.51 us
    unnamed x8, local copies, waits for them, and re-layouts  2.85 us
  transfers between devices with their start and end apart: 4, of which 4 were waited for; matrix products, arithmetic and copies ran while one was open for 4% of the time, Pallas kernels for 0%

profile of v7, /device:TPU:0, one launch (start us, length us, event | category | flops | bytes accessed | tf_op | source)
XLA Modules:
  0.0 109.8 jit_solution(3997805641588164791)
XLA Ops:
  7.2 0.0 all-gather.2.cloned.1.call-start
  7.2 2.0 %shard_map.119 = bf16[64,3712]{1,0:T(8,128)(2,1)} custom-call(bf16[128,1024]{1,0:T(8,128)(2,1)} %anc_local.1, bf16[128,1024]{1,0:T(8,128)(2,1)} %lower_hbm.1, bf16[128,1024]{1,0:T(8,128)(2,1)} %par_hbm.1, bf16[128,1024]{1,0:T(8,128)(2,1)} %ancl_hbm.1), custom_call_target="tpu_custom_call" | custom-call | tf_op jit(solution)/shard_map/pallas_call | solution.py:222
  9.2 0.0 all-gather.2.cloned.1.call-update
  9.2 0.7 convert_element_type.19
  9.9 0.7 convert_element_type.21
  10.6 0.1 broadcast_bitcast_fusion.2
  10.6 0.1 fusion
  10.7 0.1 broadcast_bitcast_fusion
  10.8 0.9 copy.19
  11.7 0.9 copy.21
  12.6 0.9 copy.17
  13.5 70.0 %all-gather.2.cloned.1.call-done.full_hbm = bf16[1024,3712]{1,0:T(8,128)(2,1)} async-done(((bf16[64,3712]{1,0:T(8,128)(2,1)}), bf16[1024,3712]{1,0:T(8,128)(2,1)}) %all-gather.2.cloned.1.call-update) | async-done | bytes 7602192 | tf_op jit(solution)/shard_map/all_gather | solution.py:228
  83.5 6.2 %shard_map.120 = (f32[128,1024]{1,0:T(8,128)}, bf16[128,512]{1,0:T(8,128)(2,1)}, bf16[128,512]{1,0:T(8,128)(2,1)}, bf16[128,512]{1,0:T(8,128)(2,1)}, f32[1,512]{1,0:T(1,128)}) custom-call(bf16[1024,1]{1,0:T(8,128)(2,1)} %bitcast.19, bf16[1024,1]{1,0:T(8,128)(2,1)} %bitcast.17, bf16[1024,1]{1,0:T(8,128)(2,1)} %bitcast.18, f32[1,512]{1,0:T(1,128)} %bitcast.23, ...), custom_call_target="tpu_custom_call" | custom-call | flops 1342177280 | bytes 4849664 | tf_op jit(solution)/shard_map/pallas_call | solution.py:233
  89.8 0.6 collective-permute-start
  90.4 3.2 %collective-permute-done = f32[1,512]{1,0:T(1,128)S(1)} collective-permute-done((f32[1,512]{1,0:T(1,128)}, f32[1,512]{1,0:T(1,128)S(1)}, u32[]{:S(2)}, u32[]{:S(2)}) %collective-permute-start) | collective-permute-done | bytes 2080 | tf_op jit(solution)/shard_map/ppermute | solution.py:270
  93.6 0.7 add.9
  94.3 1.2 %collective-permute-start.1 = (f32[1,512]{1,0:T(1,128)S(1)}, f32[1,512]{1,0:T(1,128)S(1)}, u32[]{:S(2)}, u32[]{:S(2)}) collective-permute-start(f32[1,512]{1,0:T(1,128)S(1)} %add.9), channel_id=1, source_target_pairs={{0,4},{2,6},{4,0},{6,2},{8,12},{10,14},{12,8},{14,10},{1,5},{3,7},... | collective-permute-start | bytes 6152 | tf_op jit(solution)/shard_map/ppermute | solution.py:270
  95.5 2.4 %collective-permute-done.1 = f32[1,512]{1,0:T(1,128)S(1)} collective-permute-done((f32[1,512]{1,0:T(1,128)S(1)}, f32[1,512]{1,0:T(1,128)S(1)}, u32[]{:S(2)}, u32[]{:S(2)}) %collective-permute-start.1) | collective-permute-done | bytes 2080 | tf_op jit(solution)/shard_map/ppermute | solution.py:270
  97.9 1.7 %collective-permute-start.2 = (f32[1,512]{1,0:T(1,128)S(1)}, f32[1,512]{1,0:T(1,128)S(1)}, u32[]{:S(2)}, u32[]{:S(2)}) collective-permute-start(f32[1,512]{1,0:T(1,128)S(1)} %add.10), channel_id=1, source_target_pairs={{0,8},{2,10},{4,12},{6,14},{8,0},{10,2},{12,4},{14,6},{1,9},{3,11}... | collective-permute-start | bytes 6152 | tf_op jit(solution)/shard_map/ppermute | solution.py:270
  99.6 2.8 %collective-permute-done.2 = f32[1,512]{1,0:T(1,128)S(1)} collective-permute-done((f32[1,512]{1,0:T(1,128)S(1)}, f32[1,512]{1,0:T(1,128)S(1)}, u32[]{:S(2)}, u32[]{:S(2)}) %collective-permute-start.2) | collective-permute-done | bytes 2080 | tf_op jit(solution)/shard_map/ppermute | solution.py:270
  102.4 0.6 add.11
  (4 shorter events, 0.0 us)
Async XLA Ops:
  7.2 76.4 %all-gather.2.cloned.1.call-start = ((), (), s32[]{:S(2)}) async-start(), calls=%async_computation | async-start | bytes 8077312 | tf_op jit(solution)/shard_map/all_gather | solution.py:228
  89.8 3.9 %collective-permute-start = (f32[1,512]{1,0:T(1,128)}, f32[1,512]{1,0:T(1,128)S(1)}, u32[]{:S(2)}, u32[]{:S(2)}) collective-permute-start(f32[1,512]{1,0:T(1,128)} %get-tuple-element.14), channel_id=1, source_target_pairs={{0,2},{2,0},{4,6},{6,4},{8,10},{10,8},{12,14},{14,12},{1,3},{3,1},... | collective-permute-start | bytes 6152 | tf_op jit(solution)/shard_map/ppermute | solution.py:270
  94.3 3.6 %collective-permute-start.1 = (f32[1,512]{1,0:T(1,128)S(1)}, f32[1,512]{1,0:T(1,128)S(1)}, u32[]{:S(2)}, u32[]{:S(2)}) collective-permute-start(f32[1,512]{1,0:T(1,128)S(1)} %add.9), channel_id=1, source_target_pairs={{0,4},{2,6},{4,0},{6,2},{8,12},{10,14},{12,8},{14,10},{1,5},{3,7},... | collective-permute-start | bytes 6152 | tf_op jit(solution)/shard_map/ppermute | solution.py:270
  97.9 4.5 %collective-permute-start.2 = (f32[1,512]{1,0:T(1,128)S(1)}, f32[1,512]{1,0:T(1,128)S(1)}, u32[]{:S(2)}, u32[]{:S(2)}) collective-permute-start(f32[1,512]{1,0:T(1,128)S(1)} %add.10), channel_id=1, source_target_pairs={{0,8},{2,10},{4,12},{6,14},{8,0},{10,2},{12,4},{14,6},{1,9},{3,11}... | collective-permute-start | bytes 6152 | tf_op jit(solution)/shard_map/ppermute | solution.py:270
Sparse Core Ops, SparseCore 0:
  10.9 72.6 all-gather.1

commit v8 on v6

--- a/solution.py
+++ b/solution.py
@@ -116,43 +116,56 @@
 def leaf_kernel(
     lower_gate, par_gate, anc_gate, pivots, full_hbm, anc_local, pivinv,
     block_ref, offdiag_ref, par_ref, anc_ref, part_ref,
-    sent_v, anc_v, lower_v, par_v, ancl_v, rows_v, sem,
+    anc_v, lower_v, par_v, ancl_v, rows_v, sem, anc_sem,
 ):
     row, col = lax.axis_index("row"), lax.axis_index("col")
     anc_all, order_all = anc_v.shape[0], lower_v.shape[1]
     width = par_v.shape[1]
     order_rows, anc_rows = block_ref.shape[0], anc_local.shape[0]
     off_width = offdiag_ref.shape[1]
-    sent_width = sent_v.shape[1]
+    blocks = anc_all // anc_rows
+    sent = blocks // 2 + 1
+    sent_width = sent * anc_rows
     leaf_at = sent_width + order_all
     leaf_width = (full_hbm.shape[1] - leaf_at) // 2
+    anc_copies = []
+    for p in range(blocks):
+        rows_p = pl.ds(p * anc_rows, anc_rows)
+        first = min(sent, blocks - p)
+        pieces = [(0, p, first)]
+        if first < sent:
+            pieces.append((first, 0, sent - first))
+        for src_block, dst_block, count in pieces:
+            anc_copies.append(
+                pltpu.make_async_copy(
+                    full_hbm.at[rows_p, pl.ds(src_block * anc_rows, count * anc_rows)],
+                    anc_v.at[rows_p, pl.ds(dst_block * anc_rows, count * anc_rows)],
+                    anc_sem.at[len(anc_copies)],
+                )
+            )
     copies = [
-        pltpu.make_async_copy(full_hbm.at[:, pl.ds(0, sent_width)], sent_v, sem.at[0]),
-        pltpu.make_async_copy(full_hbm.at[:, pl.ds(sent_width, order_all)], lower_v, sem.at[1]),
+        pltpu.make_async_copy(full_hbm.at[:, pl.ds(sent_width, order_all)], lower_v, sem.at[0]),
         pltpu.make_async_copy(
-            full_hbm.at[:, pl.ds(pl.multiple_of(leaf_at + col * width, 128), width)], par_v, sem.at[2]
+            full_hbm.at[:, pl.ds(pl.multiple_of(leaf_at + col * width, 128), width)], par_v, sem.at[1]
         ),
         pltpu.make_async_copy(
             full_hbm.at[:, pl.ds(pl.multiple_of(leaf_at + leaf_width + col * width, 128), width)],
             ancl_v,
-            sem.at[3],
+            sem.at[2],
         ),
     ]
-    for copy in copies:
+    for copy in anc_copies + copies:
         copy.start()
-    copies[0].wait()
-    blocks = anc_all // anc_rows
+    for copy in anc_copies:
+        copy.wait()
     for p in range(blocks):
         for q in range(blocks):
-            k = (q - p) % blocks
-            if k * anc_rows < sent_width:
-                part = sent_v[p * anc_rows : (p + 1) * anc_rows, k * anc_rows : (k + 1) * anc_rows]
-            else:
-                k = (p - q) % blocks
-                part = sent_v[q * anc_rows : (q + 1) * anc_rows, k * anc_rows : (k + 1) * anc_rows]
-                part = part.astype(jnp.float32).T.astype(jnp.bfloat16)
-            anc_v[p * anc_rows : (p + 1) * anc_rows, q * anc_rows : (q + 1) * anc_rows] = part
-    copies[1].wait()
+            if (q - p) % blocks >= sent:
+                part = anc_v[q * anc_rows : (q + 1) * anc_rows, p * anc_rows : (p + 1) * anc_rows]
+                anc_v[p * anc_rows : (p + 1) * anc_rows, q * anc_rows : (q + 1) * anc_rows] = (
+                    part.astype(jnp.float32).T.astype(jnp.bfloat16)
+                )
+    copies[0].wait()
     lower_v[...] = lower_v[...] * lower_gate[...]
     lower = lower_v[...]
     lower_cols = lower_v[:, pl.ds(pl.multiple_of(row * order_rows, 128), order_rows)]
@@ -164,8 +177,8 @@
     rows = (-jnp.dot(anc_local[...], lower, preferred_element_type=jnp.float32)).astype(jnp.bfloat16)
     rows_v[...] = rows
     offdiag_ref[...] = rows_v[:, pl.ds(pl.multiple_of(col * off_width, 128), off_width)]
+    copies[1].wait()
     copies[2].wait()
-    copies[3].wait()
     par_v[...] = par_v[...] * par_gate[...]
     ancl_v[...] = ancl_v[...] * anc_gate[...]
     par, ancl = par_v[...], ancl_v[...]
@@ -185,7 +198,8 @@
         par_own.astype(jnp.float32) * par_block.astype(jnp.float32), axis=0, keepdims=True
     ) + jnp.sum(ancl_own.astype(jnp.float32) * anc_block.astype(jnp.float32), axis=0, keepdims=True)
     part = jnp.where(row == 0, pivots[...] - part, -part)
-    part_ref[...] = jnp.broadcast_to(part, part_ref.shape)
+    for i in range(part_ref.shape[0]):
+        part_ref[i] = part
 
 
 def local_whole(
@@ -229,20 +243,20 @@
             jax.ShapeDtypeStruct((anc_rows, off_width), jnp.bfloat16),
             jax.ShapeDtypeStruct((order_rows, col_width), jnp.bfloat16),
             jax.ShapeDtypeStruct((anc_rows, col_width), jnp.bfloat16),
-            jax.ShapeDtypeStruct((row_devices, col_width), jnp.float32),
+            jax.ShapeDtypeStruct((row_devices, 1, col_width), jnp.float32),
         ),
         in_specs=[vmem] * 4
         + [pl.BlockSpec(memory_space=pl.ANY)]
         + [vmem] * 2,
         out_specs=(vmem,) * 5,
         scratch_shapes=[
-            pltpu.VMEM((anc_all, sent_width), jnp.bfloat16),
             pltpu.VMEM((anc_all, anc_all), jnp.bfloat16),
             pltpu.VMEM((anc_all, order_all), jnp.bfloat16),
             pltpu.VMEM((order_all, col_width), jnp.bfloat16),
             pltpu.VMEM((anc_all, col_width), jnp.bfloat16),
             pltpu.VMEM((anc_rows, order_all), jnp.bfloat16),
-            pltpu.SemaphoreType.DMA((4,)),
+            pltpu.SemaphoreType.DMA((3,)),
+            pltpu.SemaphoreType.DMA((2 * row_devices,)),
         ],
         cost_estimate=pl.CostEstimate(
             flops=flops, transcendentals=0, bytes_accessed=full.size + 8 * anc_rows * order_all
@@ -256,7 +270,7 @@
         anc_inverse,
         parent_pivinv,
     )
-    density = jnp.sum(lax.all_to_all(parts, "row", 0, 0), axis=0)
+    density = jnp.sum(lax.all_to_all(parts, "row", 0, 0, tiled=True), axis=0)[0]
     return block, offdiag_own, par_block, anc_block, density
 
 

time: 108 us -> 108 us (level)
  no operation moved by 1% of the time
where the time goes in v8:
time: 108 us
  waiting for transfers between devices  70 us (65%)
  between operations  14 us (13%)
  blocking collectives  9.82 us (9%)
  Pallas kernels  9.04 us (8%)
  local copies, waits for them, and re-layouts  2.93 us (3%)
  other arithmetic  1.92 us (2%)
    all_gather x1, waiting for transfers between devices, local_whole(): full = lax.all_gather(piece, ('row', 'col'), axis=0, tiled=True)  70 us
    all_to_all x1, blocking collectives, local_whole(): density = jnp.sum(lax.all_to_all(parts, 'row', 0, 0, tiled=True), axis=0)[0]  9.82 us
    pallas_call x1, Pallas kernels, local_whole(): pl.pallas_call(leaf_kernel, out_shape=(jax.ShapeDtypeStruct((order_rows,...  7.04 us
    unnamed x8, local copies, waits for them, and re-layouts  2.85 us
  transfers between devices with their start and end apart: 1, of which 1 were waited for; matrix products, arithmetic and copies ran while one was open for 4% of the time, Pallas kernels for 0%

profile of v8, /device:TPU:0, one launch (start us, length us, event | category | flops | bytes accessed | tf_op | source)
XLA Modules:
  0.0 107.8 jit_solution(10185253164244708014)
XLA Ops:
  7.2 0.0 all-gather.2.cloned.1.call-start
  7.2 2.0 %shard_map.119 = bf16[64,3712]{1,0:T(8,128)(2,1)} custom-call(bf16[128,1024]{1,0:T(8,128)(2,1)} %anc_local.1, bf16[128,1024]{1,0:T(8,128)(2,1)} %lower_hbm.1, bf16[128,1024]{1,0:T(8,128)(2,1)} %par_hbm.1, bf16[128,1024]{1,0:T(8,128)(2,1)} %ancl_hbm.1), custom_call_target="tpu_custom_call" | custom-call | tf_op jit(solution)/shard_map/pallas_call | solution.py:228
  9.2 0.0 all-gather.2.cloned.1.call-update
  9.2 0.7 convert_element_type.19
  9.9 0.7 convert_element_type.21
  10.6 0.1 broadcast_bitcast_fusion.2
  10.6 0.1 fusion
  10.7 0.1 broadcast_bitcast_fusion
  10.8 0.9 copy.19
  11.7 0.9 copy.21
  12.6 0.9 copy.17
  13.5 70.0 %all-gather.2.cloned.1.call-done.full_hbm = bf16[1024,3712]{1,0:T(8,128)(2,1)} async-done(((bf16[64,3712]{1,0:T(8,128)(2,1)}), bf16[1024,3712]{1,0:T(8,128)(2,1)}) %all-gather.2.cloned.1.call-update) | async-done | bytes 7602192 | tf_op jit(solution)/shard_map/all_gather | solution.py:234
  83.5 7.0 %shard_map.120 = (f32[128,1024]{1,0:T(8,128)}, bf16[128,512]{1,0:T(8,128)(2,1)}, bf16[128,512]{1,0:T(8,128)(2,1)}, bf16[128,512]{1,0:T(8,128)(2,1)}, f32[8,1,512]{2,1,0:T(1,128)}) custom-call(bf16[1024,1]{1,0:T(8,128)(2,1)} %bitcast.18, bf16[1024,1]{1,0:T(8,128)(2,1)} %bitcast.16, bf16[1024,1]{1,0:T(8,128)(2,1)} %bitcast.17, f32[1,512]{1,0:T(1,128)} %bitcast.22, ...), custom_call_target="tpu_custom_call" | custom-call | flops 1342177280 | bytes 4849664 | tf_op jit(solution)/shard_map/pallas_call | solution.py:239
  90.6 9.8 %all_to_all.5 = f32[8,1,512]{2,1,0:T(1,128)S(1)} all-to-all(f32[8,1,512]{2,1,0:T(1,128)} %get-tuple-element.14), channel_id=1, replica_groups=mesh['pole'=2,'row'=8,'col'=2] {'row'}, dimensions={0} | all-to-all | bytes 32768 | tf_op jit(solution)/shard_map/all_to_all | solution.py:273
  100.4 0.6 reduce_sum.9
  (3 shorter events, 0.0 us)
Async XLA Ops:
  7.2 76.4 %all-gather.2.cloned.1.call-start = ((), (), s32[]{:S(2)}) async-start(), calls=%async_computation.1 | async-start | bytes 8077312 | tf_op jit(solution)/shard_map/all_gather | solution.py:234
Sparse Core Ops, SparseCore 0:
  10.9 72.6 all-gather.1

commit v9 on v6

--- a/solution.py
+++ b/solution.py
@@ -185,7 +185,8 @@
         par_own.astype(jnp.float32) * par_block.astype(jnp.float32), axis=0, keepdims=True
     ) + jnp.sum(ancl_own.astype(jnp.float32) * anc_block.astype(jnp.float32), axis=0, keepdims=True)
     part = jnp.where(row == 0, pivots[...] - part, -part)
-    part_ref[...] = jnp.broadcast_to(part, part_ref.shape)
+    for i in range(part_ref.shape[0]):
+        part_ref[i] = part
 
 
 def local_whole(
@@ -229,7 +230,7 @@
             jax.ShapeDtypeStruct((anc_rows, off_width), jnp.bfloat16),
             jax.ShapeDtypeStruct((order_rows, col_width), jnp.bfloat16),
             jax.ShapeDtypeStruct((anc_rows, col_width), jnp.bfloat16),
-            jax.ShapeDtypeStruct((row_devices, col_width), jnp.float32),
+            jax.ShapeDtypeStruct((row_devices, 1, col_width), jnp.float32),
         ),
         in_specs=[vmem] * 4
         + [pl.BlockSpec(memory_space=pl.ANY)]
@@ -256,7 +257,7 @@
         anc_inverse,
         parent_pivinv,
     )
-    density = jnp.sum(lax.all_to_all(parts, "row", 0, 0), axis=0)
+    density = jnp.sum(lax.all_to_all(parts, "row", 0, 0, tiled=True), axis=0)[0]
     return block, offdiag_own, par_block, anc_block, density
 
 

time: 108 us -> 107 us (level)
  no operation moved by 1% of the time
where the time goes in v9:
time: 107 us
  waiting for transfers between devices  70 us (65%)
  between operations  14 us (13%)
  blocking collectives  9.82 us (9%)
  Pallas kernels  8.26 us (8%)
  local copies, waits for them, and re-layouts  2.93 us (3%)
  other arithmetic  1.92 us (2%)
    all_gather x1, waiting for transfers between devices, local_whole(): full = lax.all_gather(piece, ('row', 'col'), axis=0, tiled=True)  70 us
    all_to_all x1, blocking collectives, local_whole(): density = jnp.sum(lax.all_to_all(parts, 'row', 0, 0, tiled=True), axis=0)[0]  9.82 us
    pallas_call x1, Pallas kernels, local_whole(): pl.pallas_call(leaf_kernel, out_shape=(jax.ShapeDtypeStruct((order_rows,...  6.25 us
    unnamed x8, local copies, waits for them, and re-layouts  2.85 us
  transfers between devices with their start and end apart: 1, of which 1 were waited for; matrix products, arithmetic and copies ran while one was open for 4% of the time, Pallas kernels for 0%

profile of v9, /device:TPU:0, one launch (start us, length us, event | category | flops | bytes accessed | tf_op | source)
XLA Modules:
  0.0 107.1 jit_solution(8899877058134857656)
XLA Ops:
  7.2 0.0 all-gather.2.cloned.1.call-start
  7.2 2.0 %shard_map.119 = bf16[64,3712]{1,0:T(8,128)(2,1)} custom-call(bf16[128,1024]{1,0:T(8,128)(2,1)} %anc_local.1, bf16[128,1024]{1,0:T(8,128)(2,1)} %lower_hbm.1, bf16[128,1024]{1,0:T(8,128)(2,1)} %par_hbm.1, bf16[128,1024]{1,0:T(8,128)(2,1)} %ancl_hbm.1), custom_call_target="tpu_custom_call" | custom-call | tf_op jit(solution)/shard_map/pallas_call | solution.py:215
  9.2 0.0 all-gather.2.cloned.1.call-update
  9.2 0.7 convert_element_type.19
  9.9 0.7 convert_element_type.21
  10.6 0.1 broadcast_bitcast_fusion.2
  10.6 0.1 fusion
  10.7 0.1 broadcast_bitcast_fusion
  10.8 0.9 copy.19
  11.7 0.9 copy.21
  12.6 0.9 copy.17
  13.5 70.0 %all-gather.2.cloned.1.call-done.full_hbm = bf16[1024,3712]{1,0:T(8,128)(2,1)} async-done(((bf16[64,3712]{1,0:T(8,128)(2,1)}), bf16[1024,3712]{1,0:T(8,128)(2,1)}) %all-gather.2.cloned.1.call-update) | async-done | bytes 7602192 | tf_op jit(solution)/shard_map/all_gather | solution.py:221
  83.5 6.3 %shard_map.120 = (f32[128,1024]{1,0:T(8,128)}, bf16[128,512]{1,0:T(8,128)(2,1)}, bf16[128,512]{1,0:T(8,128)(2,1)}, bf16[128,512]{1,0:T(8,128)(2,1)}, f32[8,1,512]{2,1,0:T(1,128)}) custom-call(bf16[1024,1]{1,0:T(8,128)(2,1)} %bitcast.18, bf16[1024,1]{1,0:T(8,128)(2,1)} %bitcast.16, bf16[1024,1]{1,0:T(8,128)(2,1)} %bitcast.17, f32[1,512]{1,0:T(1,128)} %bitcast.22, ...), custom_call_target="tpu_custom_call" | custom-call | flops 1342177280 | bytes 4849664 | tf_op jit(solution)/shard_map/pallas_call | solution.py:226
  89.8 9.8 %all_to_all.5 = f32[8,1,512]{2,1,0:T(1,128)S(1)} all-to-all(f32[8,1,512]{2,1,0:T(1,128)} %get-tuple-element.14), channel_id=1, replica_groups=mesh['pole'=2,'row'=8,'col'=2] {'row'}, dimensions={0} | all-to-all | bytes 32768 | tf_op jit(solution)/shard_map/all_to_all | solution.py:260
  99.6 0.6 reduce_sum.9
  (3 shorter events, 0.0 us)
Async XLA Ops:
  7.2 76.4 %all-gather.2.cloned.1.call-start = ((), (), s32[]{:S(2)}) async-start(), calls=%async_computation.1 | async-start | bytes 8077312 | tf_op jit(solution)/shard_map/all_gather | solution.py:221
Sparse Core Ops, SparseCore 0:
  10.9 72.6 all-gather.1

commit v10 on v9

--- a/solution.py
+++ b/solution.py
@@ -127,8 +127,8 @@
     leaf_at = sent_width + order_all
     leaf_width = (full_hbm.shape[1] - leaf_at) // 2
     copies = [
+        pltpu.make_async_copy(full_hbm.at[:, pl.ds(sent_width, order_all)], lower_v, sem.at[1]),
         pltpu.make_async_copy(full_hbm.at[:, pl.ds(0, sent_width)], sent_v, sem.at[0]),
-        pltpu.make_async_copy(full_hbm.at[:, pl.ds(sent_width, order_all)], lower_v, sem.at[1]),
         pltpu.make_async_copy(
             full_hbm.at[:, pl.ds(pl.multiple_of(leaf_at + col * width, 128), width)], par_v, sem.at[2]
         ),
@@ -140,7 +140,17 @@
     ]
     for copy in copies:
         copy.start()
+    gate_row = lower_gate[...]
+    gate_col = gate_row.T
+    anc_here = anc_local[...]
     copies[0].wait()
+    lower = lower_v[...]
+    rows = (-jnp.dot(anc_here * gate_col, lower, preferred_element_type=jnp.float32)).astype(
+        jnp.bfloat16
+    )
+    rows_v[...] = rows
+    offdiag_ref[...] = rows_v[:, pl.ds(pl.multiple_of(col * off_width, 128), off_width)]
+    copies[1].wait()
     blocks = anc_all // anc_rows
     for p in range(blocks):
         for q in range(blocks):
@@ -152,18 +162,12 @@
                 part = sent_v[q * anc_rows : (q + 1) * anc_rows, k * anc_rows : (k + 1) * anc_rows]
                 part = part.astype(jnp.float32).T.astype(jnp.bfloat16)
             anc_v[p * anc_rows : (p + 1) * anc_rows, q * anc_rows : (q + 1) * anc_rows] = part
-    copies[1].wait()
-    lower_v[...] = lower_v[...] * lower_gate[...]
-    lower = lower_v[...]
-    lower_cols = lower_v[:, pl.ds(pl.multiple_of(row * order_rows, 128), order_rows)]
+    lower_cols = lower_v[:, pl.ds(pl.multiple_of(row * order_rows, 128), order_rows)] * gate_row
     offdiag_t = (
         -jnp.dot(lower_cols.T, anc_v[...], preferred_element_type=jnp.float32)
     ).astype(jnp.bfloat16)
-    block = pivinv[...] - jnp.dot(offdiag_t, lower, preferred_element_type=jnp.float32)
+    block = pivinv[...] - jnp.dot(offdiag_t * gate_col, lower, preferred_element_type=jnp.float32)
     block_ref[...] = block
-    rows = (-jnp.dot(anc_local[...], lower, preferred_element_type=jnp.float32)).astype(jnp.bfloat16)
-    rows_v[...] = rows
-    offdiag_ref[...] = rows_v[:, pl.ds(pl.multiple_of(col * off_width, 128), off_width)]
     copies[2].wait()
     copies[3].wait()
     par_v[...] = par_v[...] * par_gate[...]

time: 107 us -> 107 us (level)
  no operation moved by 1% of the time
where the time goes in v10:
time: 107 us
  waiting for transfers between devices  70 us (65%)
  between operations  14 us (13%)
  blocking collectives  9.82 us (9%)
  Pallas kernels  8.23 us (8%)
  local copies, waits for them, and re-layouts  2.93 us (3%)
  other arithmetic  1.92 us (2%)
    all_gather x1, waiting for transfers between devices, local_whole(): full = lax.all_gather(piece, ('row', 'col'), axis=0, tiled=True)  70 us
    all_to_all x1, blocking collectives, local_whole(): density = jnp.sum(lax.all_to_all(parts, 'row', 0, 0, tiled=True), axis=0)[0]  9.82 us
    pallas_call x1, Pallas kernels, local_whole(): pl.pallas_call(leaf_kernel, out_shape=(jax.ShapeDtypeStruct((order_rows,...  6.23 us
    unnamed x8, local copies, waits for them, and re-layouts  2.85 us
  transfers between devices with their start and end apart: 1, of which 1 were waited for; matrix products, arithmetic and copies ran while one was open for 4% of the time, Pallas kernels for 0%

profile of v10, /device:TPU:0, one launch (start us, length us, event | category | flops | bytes accessed | tf_op | source)
XLA Modules:
  0.0 107.0 jit_solution(1113072766847043936)
XLA Ops:
  7.2 0.0 all-gather.2.cloned.1.call-start
  7.2 2.0 %shard_map.119 = bf16[64,3712]{1,0:T(8,128)(2,1)} custom-call(bf16[128,1024]{1,0:T(8,128)(2,1)} %anc_local.1, bf16[128,1024]{1,0:T(8,128)(2,1)} %lower_hbm.1, bf16[128,1024]{1,0:T(8,128)(2,1)} %par_hbm.1, bf16[128,1024]{1,0:T(8,128)(2,1)} %ancl_hbm.1), custom_call_target="tpu_custom_call" | custom-call | tf_op jit(solution)/shard_map/pallas_call | solution.py:219
  9.2 0.0 all-gather.2.cloned.1.call-update
  9.2 0.7 convert_element_type.19
  9.9 0.7 convert_element_type.21
  10.6 0.1 broadcast_bitcast_fusion.2
  10.6 0.1 fusion
  10.7 0.1 broadcast_bitcast_fusion
  10.8 0.9 copy.19
  11.7 0.9 copy.21
  12.6 0.9 copy.17
  13.5 70.0 %all-gather.2.cloned.1.call-done.full_hbm = bf16[1024,3712]{1,0:T(8,128)(2,1)} async-done(((bf16[64,3712]{1,0:T(8,128)(2,1)}), bf16[1024,3712]{1,0:T(8,128)(2,1)}) %all-gather.2.cloned.1.call-update) | async-done | bytes 7602192 | tf_op jit(solution)/shard_map/all_gather | solution.py:225
  83.5 6.2 %shard_map.120 = (f32[128,1024]{1,0:T(8,128)}, bf16[128,512]{1,0:T(8,128)(2,1)}, bf16[128,512]{1,0:T(8,128)(2,1)}, bf16[128,512]{1,0:T(8,128)(2,1)}, f32[8,1,512]{2,1,0:T(1,128)}) custom-call(bf16[1024,1]{1,0:T(8,128)(2,1)} %bitcast.18, bf16[1024,1]{1,0:T(8,128)(2,1)} %bitcast.16, bf16[1024,1]{1,0:T(8,128)(2,1)} %bitcast.17, f32[1,512]{1,0:T(1,128)} %bitcast.22, ...), custom_call_target="tpu_custom_call" | custom-call | flops 1342177280 | bytes 4849664 | tf_op jit(solution)/shard_map/pallas_call | solution.py:230
  89.8 9.8 %all_to_all.5 = f32[8,1,512]{2,1,0:T(1,128)S(1)} all-to-all(f32[8,1,512]{2,1,0:T(1,128)} %get-tuple-element.14), channel_id=1, replica_groups=mesh['pole'=2,'row'=8,'col'=2] {'row'}, dimensions={0} | all-to-all | bytes 32768 | tf_op jit(solution)/shard_map/all_to_all | solution.py:264
  99.6 0.6 reduce_sum.9
  (3 shorter events, 0.0 us)
Async XLA Ops:
  7.2 76.4 %all-gather.2.cloned.1.call-start = ((), (), s32[]{:S(2)}) async-start(), calls=%async_computation.1 | async-start | bytes 8077312 | tf_op jit(solution)/shard_map/all_gather | solution.py:225
Sparse Core Ops, SparseCore 0:
  10.9 72.6 all-gather.1

commit v11 on v10

--- a/solution.py
+++ b/solution.py
@@ -138,12 +138,14 @@
             sem.at[3],
         ),
     ]
-    for copy in copies:
-        copy.start()
+    copies[0].start()
+    copies[1].start()
     gate_row = lower_gate[...]
     gate_col = gate_row.T
     anc_here = anc_local[...]
     copies[0].wait()
+    copies[2].start()
+    copies[3].start()
     lower = lower_v[...]
     rows = (-jnp.dot(anc_here * gate_col, lower, preferred_element_type=jnp.float32)).astype(
         jnp.bfloat16
@@ -152,16 +154,21 @@
     offdiag_ref[...] = rows_v[:, pl.ds(pl.multiple_of(col * off_width, 128), off_width)]
     copies[1].wait()
     blocks = anc_all // anc_rows
+    sent = sent_width // anc_rows
     for p in range(blocks):
+        rows_p = slice(p * anc_rows, (p + 1) * anc_rows)
+        first = min(sent, blocks - p)
+        anc_v[rows_p, p * anc_rows : (p + first) * anc_rows] = sent_v[rows_p, : first * anc_rows]
+        if first < sent:
+            anc_v[rows_p, : (sent - first) * anc_rows] = sent_v[rows_p, first * anc_rows : sent_width]
         for q in range(blocks):
             k = (q - p) % blocks
-            if k * anc_rows < sent_width:
-                part = sent_v[p * anc_rows : (p + 1) * anc_rows, k * anc_rows : (k + 1) * anc_rows]
-            else:
+            if k >= sent:
                 k = (p - q) % blocks
                 part = sent_v[q * anc_rows : (q + 1) * anc_rows, k * anc_rows : (k + 1) * anc_rows]
-                part = part.astype(jnp.float32).T.astype(jnp.bfloat16)
-            anc_v[p * anc_rows : (p + 1) * anc_rows, q * anc_rows : (q + 1) * anc_rows] = part
+                anc_v[rows_p, q * anc_rows : (q + 1) * anc_rows] = (
+                    part.astype(jnp.float32).T.astype(jnp.bfloat16)
+                )
     lower_cols = lower_v[:, pl.ds(pl.multiple_of(row * order_rows, 128), order_rows)] * gate_row
     offdiag_t = (
         -jnp.dot(lower_cols.T, anc_v[...], preferred_element_type=jnp.float32)

time: 107 us -> 107 us (level)
  no operation moved by 1% of the time
where the time goes in v11:
time: 107 us
  waiting for transfers between devices  70 us (65%)
  between operations  14 us (13%)
  blocking collectives  9.82 us (9%)
  Pallas kernels  8.23 us (8%)
  local copies, waits for them, and re-layouts  2.93 us (3%)
  other arithmetic  1.92 us (2%)
    all_gather x1, waiting for transfers between devices, local_whole(): full = lax.all_gather(piece, ('row', 'col'), axis=0, tiled=True)  70 us
    all_to_all x1, blocking collectives, local_whole(): density = jnp.sum(lax.all_to_all(parts, 'row', 0, 0, tiled=True), axis=0)[0]  9.82 us
    pallas_call x1, Pallas kernels, local_whole(): pl.pallas_call(leaf_kernel, out_shape=(jax.ShapeDtypeStruct((order_rows,...  6.22 us
    unnamed x8, local copies, waits for them, and re-layouts  2.85 us
  transfers between devices with their start and end apart: 1, of which 1 were waited for; matrix products, arithmetic and copies ran while one was open for 4% of the time, Pallas kernels for 0%

profile of v11, /device:TPU:0, one launch (start us, length us, event | category | flops | bytes accessed | tf_op | source)
XLA Modules:
  0.0 107.0 jit_solution(3956569881466059904)
XLA Ops:
  7.2 0.0 all-gather.2.cloned.1.call-start
  7.2 2.0 %shard_map.119 = bf16[64,3712]{1,0:T(8,128)(2,1)} custom-call(bf16[128,1024]{1,0:T(8,128)(2,1)} %anc_local.1, bf16[128,1024]{1,0:T(8,128)(2,1)} %lower_hbm.1, bf16[128,1024]{1,0:T(8,128)(2,1)} %par_hbm.1, bf16[128,1024]{1,0:T(8,128)(2,1)} %ancl_hbm.1), custom_call_target="tpu_custom_call" | custom-call | tf_op jit(solution)/shard_map/pallas_call | solution.py:226
  9.2 0.0 all-gather.2.cloned.1.call-update
  9.2 0.7 convert_element_type.19
  9.9 0.7 convert_element_type.21
  10.6 0.1 broadcast_bitcast_fusion.2
  10.6 0.1 fusion
  10.7 0.1 broadcast_bitcast_fusion
  10.8 0.9 copy.19
  11.7 0.9 copy.21
  12.6 0.9 copy.17
  13.5 70.0 %all-gather.2.cloned.1.call-done.full_hbm = bf16[1024,3712]{1,0:T(8,128)(2,1)} async-done(((bf16[64,3712]{1,0:T(8,128)(2,1)}), bf16[1024,3712]{1,0:T(8,128)(2,1)}) %all-gather.2.cloned.1.call-update) | async-done | bytes 7602192 | tf_op jit(solution)/shard_map/all_gather | solution.py:232
  83.5 6.2 %shard_map.120 = (f32[128,1024]{1,0:T(8,128)}, bf16[128,512]{1,0:T(8,128)(2,1)}, bf16[128,512]{1,0:T(8,128)(2,1)}, bf16[128,512]{1,0:T(8,128)(2,1)}, f32[8,1,512]{2,1,0:T(1,128)}) custom-call(bf16[1024,1]{1,0:T(8,128)(2,1)} %bitcast.18, bf16[1024,1]{1,0:T(8,128)(2,1)} %bitcast.16, bf16[1024,1]{1,0:T(8,128)(2,1)} %bitcast.17, f32[1,512]{1,0:T(1,128)} %bitcast.22, ...), custom_call_target="tpu_custom_call" | custom-call | flops 1342177280 | bytes 4849664 | tf_op jit(solution)/shard_map/pallas_call | solution.py:237
  89.8 9.8 %all_to_all.5 = f32[8,1,512]{2,1,0:T(1,128)S(1)} all-to-all(f32[8,1,512]{2,1,0:T(1,128)} %get-tuple-element.14), channel_id=1, replica_groups=mesh['pole'=2,'row'=8,'col'=2] {'row'}, dimensions={0} | all-to-all | bytes 32768 | tf_op jit(solution)/shard_map/all_to_all | solution.py:271
  99.6 0.6 reduce_sum.9
  (3 shorter events, 0.0 us)
Async XLA Ops:
  7.2 76.4 %all-gather.2.cloned.1.call-start = ((), (), s32[]{:S(2)}) async-start(), calls=%async_computation.1 | async-start | bytes 8077312 | tf_op jit(solution)/shard_map/all_gather | solution.py:232
Sparse Core Ops, SparseCore 0:
  10.9 72.6 all-gather.1

commit v12 on v11

--- a/solution.py
+++ b/solution.py
@@ -126,33 +126,17 @@
     sent_width = sent_v.shape[1]
     leaf_at = sent_width + order_all
     leaf_width = (full_hbm.shape[1] - leaf_at) // 2
-    copies = [
-        pltpu.make_async_copy(full_hbm.at[:, pl.ds(sent_width, order_all)], lower_v, sem.at[1]),
-        pltpu.make_async_copy(full_hbm.at[:, pl.ds(0, sent_width)], sent_v, sem.at[0]),
-        pltpu.make_async_copy(
-            full_hbm.at[:, pl.ds(pl.multiple_of(leaf_at + col * width, 128), width)], par_v, sem.at[2]
-        ),
-        pltpu.make_async_copy(
-            full_hbm.at[:, pl.ds(pl.multiple_of(leaf_at + leaf_width + col * width, 128), width)],
-            ancl_v,
-            sem.at[3],
-        ),
-    ]
-    copies[0].start()
-    copies[1].start()
+    lower_v[...] = full_hbm[:, sent_width : sent_width + order_all]
     gate_row = lower_gate[...]
     gate_col = gate_row.T
     anc_here = anc_local[...]
-    copies[0].wait()
-    copies[2].start()
-    copies[3].start()
     lower = lower_v[...]
     rows = (-jnp.dot(anc_here * gate_col, lower, preferred_element_type=jnp.float32)).astype(
         jnp.bfloat16
     )
     rows_v[...] = rows
     offdiag_ref[...] = rows_v[:, pl.ds(pl.multiple_of(col * off_width, 128), off_width)]
-    copies[1].wait()
+    sent_v[...] = full_hbm[:, :sent_width]
     blocks = anc_all // anc_rows
     sent = sent_width // anc_rows
     for p in range(blocks):
@@ -175,10 +159,11 @@
     ).astype(jnp.bfloat16)
     block = pivinv[...] - jnp.dot(offdiag_t * gate_col, lower, preferred_element_type=jnp.float32)
     block_ref[...] = block
-    copies[2].wait()
-    copies[3].wait()
-    par_v[...] = par_v[...] * par_gate[...]
-    ancl_v[...] = ancl_v[...] * anc_gate[...]
+    par_v[...] = full_hbm[:, pl.ds(pl.multiple_of(leaf_at + col * width, 128), width)] * par_gate[...]
+    ancl_v[...] = (
+        full_hbm[:, pl.ds(pl.multiple_of(leaf_at + leaf_width + col * width, 128), width)]
+        * anc_gate[...]
+    )
     par, ancl = par_v[...], ancl_v[...]
     upper = jnp.dot(
         block.astype(jnp.bfloat16), par, preferred_element_type=jnp.float32
@@ -243,9 +228,7 @@
             jax.ShapeDtypeStruct((anc_rows, col_width), jnp.bfloat16),
             jax.ShapeDtypeStruct((row_devices, 1, col_width), jnp.float32),
         ),
-        in_specs=[vmem] * 4
-        + [pl.BlockSpec(memory_space=pl.ANY)]
-        + [vmem] * 2,
+        in_specs=[vmem] * 7,
         out_specs=(vmem,) * 5,
         scratch_shapes=[
             pltpu.VMEM((anc_all, sent_width), jnp.bfloat16),

time: 107 us -> 107 us (level)
  no operation moved by 1% of the time
where the time goes in v12:
time: 107 us
  waiting for transfers between devices  70 us (65%)
  between operations  14 us (13%)
  blocking collectives  9.82 us (9%)
  Pallas kernels  8.35 us (8%)
  local copies, waits for them, and re-layouts  2.93 us (3%)
  other arithmetic  1.92 us (2%)
    all_gather x1, waiting for transfers between devices, local_whole(): full = lax.all_gather(piece, ('row', 'col'), axis=0, tiled=True)  70 us
    all_to_all x1, blocking collectives, local_whole(): density = jnp.sum(lax.all_to_all(parts, 'row', 0, 0, tiled=True), axis=0)[0]  9.82 us
    pallas_call x1, Pallas kernels, local_whole(): pl.pallas_call(leaf_kernel, out_shape=(jax.ShapeDtypeStruct((order_rows,...  6.34 us
    unnamed x8, local copies, waits for them, and re-layouts  2.85 us
  transfers between devices with their start and end apart: 1, of which 1 were waited for; matrix products, arithmetic and copies ran while one was open for 4% of the time, Pallas kernels for 0%

profile of v12, /device:TPU:0, one launch (start us, length us, event | category | flops | bytes accessed | tf_op | source)
XLA Modules:
  0.0 107.1 jit_solution(11990897359205785703)
XLA Ops:
  7.2 0.0 all-gather.2.cloned.1.call-start
  7.2 2.0 %shard_map.119 = bf16[64,3712]{1,0:T(8,128)(2,1)} custom-call(bf16[128,1024]{1,0:T(8,128)(2,1)} %anc_local.1, bf16[128,1024]{1,0:T(8,128)(2,1)} %lower_hbm.1, bf16[128,1024]{1,0:T(8,128)(2,1)} %par_hbm.1, bf16[128,1024]{1,0:T(8,128)(2,1)} %ancl_hbm.1), custom_call_target="tpu_custom_call" | custom-call | tf_op jit(solution)/shard_map/pallas_call | solution.py:211
  9.2 0.0 all-gather.2.cloned.1.call-update
  9.2 0.7 convert_element_type.19
  9.9 0.7 convert_element_type.21
  10.6 0.1 broadcast_bitcast_fusion.2
  10.6 0.1 fusion
  10.7 0.1 broadcast_bitcast_fusion
  10.8 0.9 copy.19
  11.7 0.9 copy.21
  12.6 0.9 copy.17
  13.5 70.0 %all-gather.2.cloned.1.call-done.full_hbm = bf16[1024,3712]{1,0:T(8,128)(2,1)} async-done(((bf16[64,3712]{1,0:T(8,128)(2,1)}), bf16[1024,3712]{1,0:T(8,128)(2,1)}) %all-gather.2.cloned.1.call-update) | async-done | bytes 7602192 | tf_op jit(solution)/shard_map/all_gather | solution.py:217
  83.5 6.3 %shard_map.120 = (f32[128,1024]{1,0:T(8,128)}, bf16[128,512]{1,0:T(8,128)(2,1)}, bf16[128,512]{1,0:T(8,128)(2,1)}, bf16[128,512]{1,0:T(8,128)(2,1)}, f32[8,1,512]{2,1,0:T(1,128)}) custom-call(bf16[1024,1]{1,0:T(8,128)(2,1)} %bitcast.18, bf16[1024,1]{1,0:T(8,128)(2,1)} %bitcast.16, bf16[1024,1]{1,0:T(8,128)(2,1)} %bitcast.17, f32[1,512]{1,0:T(1,128)} %bitcast.22, ...), custom_call_target="tpu_custom_call" | custom-call | flops 1342177280 | bytes 4849664 | tf_op jit(solution)/shard_map/pallas_call | solution.py:222
  89.9 9.8 %all_to_all.5 = f32[8,1,512]{2,1,0:T(1,128)S(1)} all-to-all(f32[8,1,512]{2,1,0:T(1,128)} %get-tuple-element.14), channel_id=1, replica_groups=mesh['pole'=2,'row'=8,'col'=2] {'row'}, dimensions={0} | all-to-all | bytes 32768 | tf_op jit(solution)/shard_map/all_to_all | solution.py:254
  99.7 0.6 reduce_sum.9
  (3 shorter events, 0.0 us)
Async XLA Ops:
  7.2 76.4 %all-gather.2.cloned.1.call-start = ((), (), s32[]{:S(2)}) async-start(), calls=%async_computation.1 | async-start | bytes 8077312 | tf_op jit(solution)/shard_map/all_gather | solution.py:217
Sparse Core Ops, SparseCore 0:
  10.9 72.6 all-gather.1

commit v13 on v12

--- a/solution.py
+++ b/solution.py
@@ -126,17 +126,42 @@
     sent_width = sent_v.shape[1]
     leaf_at = sent_width + order_all
     leaf_width = (full_hbm.shape[1] - leaf_at) // 2
-    lower_v[...] = full_hbm[:, sent_width : sent_width + order_all]
+    chunks = 4
+    step = anc_all // chunks
+    windows = [
+        (pl.ds(sent_width, order_all), lower_v),
+        (pl.ds(0, sent_width), sent_v),
+        (pl.ds(pl.multiple_of(leaf_at + col * width, 128), width), par_v),
+        (pl.ds(pl.multiple_of(leaf_at + leaf_width + col * width, 128), width), ancl_v),
+    ]
+    copies = [
+        [
+            pltpu.make_async_copy(
+                full_hbm.at[pl.ds(i * step, step), cols],
+                target.at[pl.ds(i * step, step), :],
+                sem.at[j * chunks + i],
+            )
+            for i in range(chunks)
+        ]
+        for j, (cols, target) in enumerate(windows)
+    ]
+    for copy in copies[0] + copies[1]:
+        copy.start()
     gate_row = lower_gate[...]
     gate_col = gate_row.T
     anc_here = anc_local[...]
+    for copy in copies[0]:
+        copy.wait()
+    for copy in copies[2] + copies[3]:
+        copy.start()
     lower = lower_v[...]
     rows = (-jnp.dot(anc_here * gate_col, lower, preferred_element_type=jnp.float32)).astype(
         jnp.bfloat16
     )
     rows_v[...] = rows
     offdiag_ref[...] = rows_v[:, pl.ds(pl.multiple_of(col * off_width, 128), off_width)]
-    sent_v[...] = full_hbm[:, :sent_width]
+    for copy in copies[1]:
+        copy.wait()
     blocks = anc_all // anc_rows
     sent = sent_width // anc_rows
     for p in range(blocks):
@@ -159,11 +184,10 @@
     ).astype(jnp.bfloat16)
     block = pivinv[...] - jnp.dot(offdiag_t * gate_col, lower, preferred_element_type=jnp.float32)
     block_ref[...] = block
-    par_v[...] = full_hbm[:, pl.ds(pl.multiple_of(leaf_at + col * width, 128), width)] * par_gate[...]
-    ancl_v[...] = (
-        full_hbm[:, pl.ds(pl.multiple_of(leaf_at + leaf_width + col * width, 128), width)]
-        * anc_gate[...]
-    )
+    for copy in copies[2] + copies[3]:
+        copy.wait()
+    par_v[...] = par_v[...] * par_gate[...]
+    ancl_v[...] = ancl_v[...] * anc_gate[...]
     par, ancl = par_v[...], ancl_v[...]
     upper = jnp.dot(
         block.astype(jnp.bfloat16), par, preferred_element_type=jnp.float32
@@ -228,7 +252,9 @@
             jax.ShapeDtypeStruct((anc_rows, col_width), jnp.bfloat16),
             jax.ShapeDtypeStruct((row_devices, 1, col_width), jnp.float32),
         ),
-        in_specs=[vmem] * 7,
+        in_specs=[vmem] * 4
+        + [pl.BlockSpec(memory_space=pl.ANY)]
+        + [vmem] * 2,
         out_specs=(vmem,) * 5,
         scratch_shapes=[
             pltpu.VMEM((anc_all, sent_width), jnp.bfloat16),
@@ -237,7 +263,7 @@
             pltpu.VMEM((order_all, col_width), jnp.bfloat16),
             pltpu.VMEM((anc_all, col_width), jnp.bfloat16),
             pltpu.VMEM((anc_rows, order_all), jnp.bfloat16),
-            pltpu.SemaphoreType.DMA((4,)),
+            pltpu.SemaphoreType.DMA((16,)),
         ],
         cost_estimate=pl.CostEstimate(
             flops=flops, transcendentals=0, bytes_accessed=full.size + 8 * anc_rows * order_all

time: 107 us -> 107 us (level)
  no operation moved by 1% of the time
where the time goes in v13:
time: 107 us
  waiting for transfers between devices  70 us (65%)
  between operations  14 us (13%)
  blocking collectives  9.82 us (9%)
  Pallas kernels  8.28 us (8%)
  local copies, waits for them, and re-layouts  2.93 us (3%)
  other arithmetic  1.92 us (2%)
    all_gather x1, waiting for transfers between devices, local_whole(): full = lax.all_gather(piece, ('row', 'col'), axis=0, tiled=True)  70 us
    all_to_all x1, blocking collectives, local_whole(): density = jnp.sum(lax.all_to_all(parts, 'row', 0, 0, tiled=True), axis=0)[0]  9.82 us
    pallas_call x1, Pallas kernels, local_whole(): pl.pallas_call(leaf_kernel, out_shape=(jax.ShapeDtypeStruct((order_rows,...  6.28 us
    unnamed x8, local copies, waits for them, and re-layouts  2.85 us
  transfers between devices with their start and end apart: 1, of which 1 were waited for; matrix products, arithmetic and copies ran while one was open for 4% of the time, Pallas kernels for 0%

profile of v13, /device:TPU:0, one launch (start us, length us, event | category | flops | bytes accessed | tf_op | source)
XLA Modules:
  0.0 107.1 jit_solution(5997551737498860401)
XLA Ops:
  7.2 0.0 all-gather.2.cloned.1.call-start
  7.2 2.0 %shard_map.119 = bf16[64,3712]{1,0:T(8,128)(2,1)} custom-call(bf16[128,1024]{1,0:T(8,128)(2,1)} %anc_local.1, bf16[128,1024]{1,0:T(8,128)(2,1)} %lower_hbm.1, bf16[128,1024]{1,0:T(8,128)(2,1)} %par_hbm.1, bf16[128,1024]{1,0:T(8,128)(2,1)} %ancl_hbm.1), custom_call_target="tpu_custom_call" | custom-call | tf_op jit(solution)/shard_map/pallas_call | solution.py:235
  9.2 0.0 all-gather.2.cloned.1.call-update
  9.2 0.7 convert_element_type.19
  9.9 0.7 convert_element_type.21
  10.6 0.1 broadcast_bitcast_fusion.2
  10.6 0.1 fusion
  10.7 0.1 broadcast_bitcast_fusion
  10.8 0.9 copy.19
  11.7 0.9 copy.21
  12.6 0.9 copy.17
  13.5 70.0 %all-gather.2.cloned.1.call-done.full_hbm = bf16[1024,3712]{1,0:T(8,128)(2,1)} async-done(((bf16[64,3712]{1,0:T(8,128)(2,1)}), bf16[1024,3712]{1,0:T(8,128)(2,1)}) %all-gather.2.cloned.1.call-update) | async-done | bytes 7602192 | tf_op jit(solution)/shard_map/all_gather | solution.py:241
  83.5 6.3 %shard_map.120 = (f32[128,1024]{1,0:T(8,128)}, bf16[128,512]{1,0:T(8,128)(2,1)}, bf16[128,512]{1,0:T(8,128)(2,1)}, bf16[128,512]{1,0:T(8,128)(2,1)}, f32[8,1,512]{2,1,0:T(1,128)}) custom-call(bf16[1024,1]{1,0:T(8,128)(2,1)} %bitcast.18, bf16[1024,1]{1,0:T(8,128)(2,1)} %bitcast.16, bf16[1024,1]{1,0:T(8,128)(2,1)} %bitcast.17, f32[1,512]{1,0:T(1,128)} %bitcast.22, ...), custom_call_target="tpu_custom_call" | custom-call | flops 1342177280 | bytes 4849664 | tf_op jit(solution)/shard_map/pallas_call | solution.py:246
  89.8 9.8 %all_to_all.5 = f32[8,1,512]{2,1,0:T(1,128)S(1)} all-to-all(f32[8,1,512]{2,1,0:T(1,128)} %get-tuple-element.14), channel_id=1, replica_groups=mesh['pole'=2,'row'=8,'col'=2] {'row'}, dimensions={0} | all-to-all | bytes 32768 | tf_op jit(solution)/shard_map/all_to_all | solution.py:280
  99.6 0.6 reduce_sum.9
  (3 shorter events, 0.0 us)
Async XLA Ops:
  7.2 76.4 %all-gather.2.cloned.1.call-start = ((), (), s32[]{:S(2)}) async-start(), calls=%async_computation.1 | async-start | bytes 8077312 | tf_op jit(solution)/shard_map/all_gather | solution.py:241
Sparse Core Ops, SparseCore 0:
  10.9 72.6 all-gather.1

commit v14 on v11

--- a/solution.py
+++ b/solution.py
@@ -114,7 +114,7 @@
 
 
 def leaf_kernel(
-    lower_gate, par_gate, anc_gate, pivots, full_hbm, anc_local, pivinv,
+    gate_col, par_col_ref, anc_col_ref, par_own_gate, anc_own_gate, pivots, full_hbm, anc_local, pivinv,
     block_ref, offdiag_ref, par_ref, anc_ref, part_ref,
     sent_v, anc_v, lower_v, par_v, ancl_v, rows_v, sem,
 ):
@@ -140,8 +140,7 @@
     ]
     copies[0].start()
     copies[1].start()
-    gate_row = lower_gate[...]
-    gate_col = gate_row.T
+    gate_col = gate_col[...]
     anc_here = anc_local[...]
     copies[0].wait()
     copies[2].start()
@@ -169,29 +168,28 @@
                 anc_v[rows_p, q * anc_rows : (q + 1) * anc_rows] = (
                     part.astype(jnp.float32).T.astype(jnp.bfloat16)
                 )
-    lower_cols = lower_v[:, pl.ds(pl.multiple_of(row * order_rows, 128), order_rows)] * gate_row
+    lower_cols = lower_v[:, pl.ds(pl.multiple_of(row * order_rows, 128), order_rows)]
     offdiag_t = (
-        -jnp.dot(lower_cols.T, anc_v[...], preferred_element_type=jnp.float32)
+        -jnp.dot(lower_cols.T * gate_col, anc_v[...], preferred_element_type=jnp.float32)
     ).astype(jnp.bfloat16)
     block = pivinv[...] - jnp.dot(offdiag_t * gate_col, lower, preferred_element_type=jnp.float32)
     block_ref[...] = block
     copies[2].wait()
     copies[3].wait()
-    par_v[...] = par_v[...] * par_gate[...]
-    ancl_v[...] = ancl_v[...] * anc_gate[...]
+    par_col, anc_col = par_col_ref[...], anc_col_ref[...]
     par, ancl = par_v[...], ancl_v[...]
     upper = jnp.dot(
-        block.astype(jnp.bfloat16), par, preferred_element_type=jnp.float32
-    ) + jnp.dot(offdiag_t, ancl, preferred_element_type=jnp.float32)
+        block.astype(jnp.bfloat16) * par_col, par, preferred_element_type=jnp.float32
+    ) + jnp.dot(offdiag_t * anc_col, ancl, preferred_element_type=jnp.float32)
     par_block = (-upper).astype(jnp.bfloat16)
-    lower_sum = jnp.dot(rows, par, preferred_element_type=jnp.float32) + jnp.dot(
-        anc_local[...], ancl, preferred_element_type=jnp.float32
+    lower_sum = jnp.dot(rows * par_col, par, preferred_element_type=jnp.float32) + jnp.dot(
+        anc_here * anc_col, ancl, preferred_element_type=jnp.float32
     )
     anc_block = (-lower_sum).astype(jnp.bfloat16)
     par_ref[...] = par_block
     anc_ref[...] = anc_block
-    par_own = par_v[pl.ds(pl.multiple_of(row * order_rows, 8), order_rows), :]
-    ancl_own = ancl_v[pl.ds(pl.multiple_of(row * anc_rows, 8), anc_rows), :]
+    par_own = par_v[pl.ds(pl.multiple_of(row * order_rows, 8), order_rows), :] * par_own_gate[...]
+    ancl_own = ancl_v[pl.ds(pl.multiple_of(row * anc_rows, 8), anc_rows), :] * anc_own_gate[...]
     part = jnp.sum(
         par_own.astype(jnp.float32) * par_block.astype(jnp.float32), axis=0, keepdims=True
     ) + jnp.sum(ancl_own.astype(jnp.float32) * anc_block.astype(jnp.float32), axis=0, keepdims=True)
@@ -243,7 +241,7 @@
             jax.ShapeDtypeStruct((anc_rows, col_width), jnp.bfloat16),
             jax.ShapeDtypeStruct((row_devices, 1, col_width), jnp.float32),
         ),
-        in_specs=[vmem] * 4
+        in_specs=[vmem] * 6
         + [pl.BlockSpec(memory_space=pl.ANY)]
         + [vmem] * 2,
         out_specs=(vmem,) * 5,
@@ -260,9 +258,11 @@
             flops=flops, transcendentals=0, bytes_accessed=full.size + 8 * anc_rows * order_all
         ),
     )(
-        parent_gate,
-        leaf_gate[:order_all],
-        leaf_gate[order_all:],
+        parent_gate.T,
+        leaf_gate[:order_all].T,
+        leaf_gate[order_all:].T,
+        lax.dynamic_slice_in_dim(leaf_gate[:order_all], row_index * order_rows, order_rows),
+        lax.dynamic_slice_in_dim(leaf_gate[order_all:], row_index * anc_rows, anc_rows),
         leaf_pivots[None, :],
         full,
         anc_inverse,

time: 107 us -> 107 us (level)
    dynamic_slice x0 -> x4, local copies, waits for them, and re-layouts: none -> 1.59 us  [the longest x2 0.8 us: local_whole(): lax.dynamic_slice_in_dim(leaf_gate[order_all:], row_index * anc_rows, anc...]
    unnamed x8 -> x7, local copies, waits for them, and re-layouts: 2.85 us -> 1.95 us
  transfers between devices with their start and end apart: 1 -> 1, of which waited for: 1 -> 1; matrix products, arithmetic and copies ran while one was open for 4% -> 5% of each run, Pallas kernels for 0% -> 0%
where the time goes in v14:
time: 107 us
  waiting for transfers between devices  69.4 us (65%)
  between operations  14.1 us (13%)
  blocking collectives  9.83 us (9%)
  Pallas kernels  7.86 us (7%)
  local copies, waits for them, and re-layouts  3.61 us (3%)
  other arithmetic  1.92 us (2%)
    all_gather x1, waiting for transfers between devices, local_whole(): full = lax.all_gather(piece, ('row', 'col'), axis=0, tiled=True)  69.4 us
    all_to_all x1, blocking collectives, local_whole(): density = jnp.sum(lax.all_to_all(parts, 'row', 0, 0, tiled=True), axis=0)[0]  9.83 us
    pallas_call x1, Pallas kernels, local_whole(): pl.pallas_call(leaf_kernel, out_shape=(jax.ShapeDtypeStruct((order_rows,...  5.86 us
  transfers between devices with their start and end apart: 1, of which 1 were waited for; matrix products, arithmetic and copies ran while one was open for 5% of the time, Pallas kernels for 0%

profile of v14, /device:TPU:0, one launch (start us, length us, event | category | flops | bytes accessed | tf_op | source)
XLA Modules:
  0.0 106.7 jit_solution(4984869855462078518)
XLA Ops:
  7.2 0.0 all-gather.2.cloned.1.call-start
  7.2 2.0 %shard_map.119 = bf16[64,3712]{1,0:T(8,128)(2,1)} custom-call(bf16[128,1024]{1,0:T(8,128)(2,1)} %anc_local.1, bf16[128,1024]{1,0:T(8,128)(2,1)} %lower_hbm.1, bf16[128,1024]{1,0:T(8,128)(2,1)} %par_hbm.1, bf16[128,1024]{1,0:T(8,128)(2,1)} %ancl_hbm.1), custom_call_target="tpu_custom_call" | custom-call | tf_op jit(solution)/shard_map/pallas_call | solution.py:224
  9.2 0.0 all-gather.2.cloned.1.call-update
  9.2 0.7 convert_element_type.19
  9.9 0.7 convert_element_type.21
  10.6 0.1 broadcast_bitcast_fusion
  10.6 0.6 copy.15
  11.2 0.1 fusion
  11.3 0.1 broadcast_bitcast_fusion.1
  11.4 0.6 copy.17
  12.0 0.6 copy.16
  12.6 0.1 dynamic-slice_bitcast_fusion.1
  12.7 0.7 copy.13.par_own_gate
  13.4 0.1 dynamic-slice_bitcast_fusion
  13.5 0.7 copy.14.anc_own_gate
  14.2 69.4 %all-gather.2.cloned.1.call-done.full_hbm = bf16[1024,3712]{1,0:T(8,128)(2,1)} async-done(((bf16[64,3712]{1,0:T(8,128)(2,1)}), bf16[1024,3712]{1,0:T(8,128)(2,1)}) %all-gather.2.cloned.1.call-update) | async-done | bytes 7602192 | tf_op jit(solution)/shard_map/all_gather | solution.py:230
  83.5 5.9 %shard_map.120 = (f32[128,1024]{1,0:T(8,128)}, bf16[128,512]{1,0:T(8,128)(2,1)}, bf16[128,512]{1,0:T(8,128)(2,1)}, bf16[128,512]{1,0:T(8,128)(2,1)}, f32[8,1,512]{2,1,0:T(1,128)}) custom-call(bf16[1,1024]{1,0:T(2,128)(2,1)} %bitcast.23, bf16[1,1024]{1,0:T(2,128)(2,1)} %bitcast.25, bf16[1,1024]{1,0:T(2,128)(2,1)} %bitcast.24, ...), custom_call_target="tpu_custom_call" | custom-call | flops 1342177280 | bytes 4849664 | tf_op jit(solution)/shard_map/pallas_call | solution.py:235
  89.4 9.8 %all_to_all.5 = f32[8,1,512]{2,1,0:T(1,128)S(1)} all-to-all(f32[8,1,512]{2,1,0:T(1,128)} %get-tuple-element.14), channel_id=1, replica_groups=mesh['pole'=2,'row'=8,'col'=2] {'row'}, dimensions={0} | all-to-all | bytes 32768 | tf_op jit(solution)/shard_map/all_to_all | solution.py:271
  99.2 0.6 reduce_sum.9
  (2 shorter events, 0.0 us)
Async XLA Ops:
  7.2 76.4 %all-gather.2.cloned.1.call-start = ((), (), s32[]{:S(2)}) async-start(), calls=%async_computation.1 | async-start | bytes 8077312 | tf_op jit(solution)/shard_map/all_gather | solution.py:230
Sparse Core Ops, SparseCore 0:
  10.9 72.6 all-gather.1

commit v15 on v14

--- a/solution.py
+++ b/solution.py
@@ -116,7 +116,7 @@
 def leaf_kernel(
     gate_col, par_col_ref, anc_col_ref, par_own_gate, anc_own_gate, pivots, full_hbm, anc_local, pivinv,
     block_ref, offdiag_ref, par_ref, anc_ref, part_ref,
-    sent_v, anc_v, lower_v, par_v, ancl_v, rows_v, sem,
+    sent_v, anc_v, lower_v, par_v, ancl_v, rows_v, pivinv_v, sem,
 ):
     row, col = lax.axis_index("row"), lax.axis_index("col")
     anc_all, order_all = anc_v.shape[0], lower_v.shape[1]
@@ -138,6 +138,8 @@
             sem.at[3],
         ),
     ]
+    pivinv_copy = pltpu.make_async_copy(pivinv, pivinv_v, sem.at[4])
+    pivinv_copy.start()
     copies[0].start()
     copies[1].start()
     gate_col = gate_col[...]
@@ -172,7 +174,8 @@
     offdiag_t = (
         -jnp.dot(lower_cols.T * gate_col, anc_v[...], preferred_element_type=jnp.float32)
     ).astype(jnp.bfloat16)
-    block = pivinv[...] - jnp.dot(offdiag_t * gate_col, lower, preferred_element_type=jnp.float32)
+    pivinv_copy.wait()
+    block = pivinv_v[...] - jnp.dot(offdiag_t * gate_col, lower, preferred_element_type=jnp.float32)
     block_ref[...] = block
     copies[2].wait()
     copies[3].wait()
@@ -242,8 +245,7 @@
             jax.ShapeDtypeStruct((row_devices, 1, col_width), jnp.float32),
         ),
         in_specs=[vmem] * 6
-        + [pl.BlockSpec(memory_space=pl.ANY)]
-        + [vmem] * 2,
+        + [pl.BlockSpec(memory_space=pl.ANY), vmem, pl.BlockSpec(memory_space=pl.ANY)],
         out_specs=(vmem,) * 5,
         scratch_shapes=[
             pltpu.VMEM((anc_all, sent_width), jnp.bfloat16),
@@ -252,7 +254,8 @@
             pltpu.VMEM((order_all, col_width), jnp.bfloat16),
             pltpu.VMEM((anc_all, col_width), jnp.bfloat16),
             pltpu.VMEM((anc_rows, order_all), jnp.bfloat16),
-            pltpu.SemaphoreType.DMA((4,)),
+            pltpu.VMEM((order_rows, order_all), jnp.float32),
+            pltpu.SemaphoreType.DMA((5,)),
         ],
         cost_estimate=pl.CostEstimate(
             flops=flops, transcendentals=0, bytes_accessed=full.size + 8 * anc_rows * order_all

time: 107 us -> 107 us (level)
  no operation moved by 1% of the time
where the time goes in v15:
time: 107 us
  waiting for transfers between devices  69.4 us (65%)
  between operations  14.1 us (13%)
  blocking collectives  9.83 us (9%)
  Pallas kernels  7.9 us (7%)
  local copies, waits for them, and re-layouts  3.61 us (3%)
  other arithmetic  1.92 us (2%)
    all_gather x1, waiting for transfers between devices, local_whole(): full = lax.all_gather(piece, ('row', 'col'), axis=0, tiled=True)  69.4 us
    all_to_all x1, blocking collectives, local_whole(): density = jnp.sum(lax.all_to_all(parts, 'row', 0, 0, tiled=True), axis=0)[0]  9.83 us
    pallas_call x1, Pallas kernels, local_whole(): pl.pallas_call(leaf_kernel, out_shape=(jax.ShapeDtypeStruct((order_rows,...  5.9 us
  transfers between devices with their start and end apart: 1, of which 1 were waited for; matrix products, arithmetic and copies ran while one was open for 5% of the time, Pallas kernels for 0%

profile of v15, /device:TPU:0, one launch (start us, length us, event | category | flops | bytes accessed | tf_op | source)
XLA Modules:
  0.0 106.7 jit_solution(9562778668662024397)
XLA Ops:
  7.2 0.0 all-gather.2.cloned.1.call-start
  7.2 2.0 %shard_map.119 = bf16[64,3712]{1,0:T(8,128)(2,1)} custom-call(bf16[128,1024]{1,0:T(8,128)(2,1)} %anc_local.1, bf16[128,1024]{1,0:T(8,128)(2,1)} %lower_hbm.1, bf16[128,1024]{1,0:T(8,128)(2,1)} %par_hbm.1, bf16[128,1024]{1,0:T(8,128)(2,1)} %ancl_hbm.1), custom_call_target="tpu_custom_call" | custom-call | tf_op jit(solution)/shard_map/pallas_call | solution.py:227
  9.2 0.0 all-gather.2.cloned.1.call-update
  9.2 0.7 convert_element_type.19
  9.9 0.7 convert_element_type.21
  10.6 0.1 broadcast_bitcast_fusion
  10.6 0.6 copy.15
  11.2 0.1 fusion
  11.3 0.1 broadcast_bitcast_fusion.1
  11.4 0.6 copy.17
  12.0 0.6 copy.16
  12.6 0.1 dynamic-slice_bitcast_fusion.1
  12.7 0.7 copy.13.par_own_gate
  13.4 0.1 dynamic-slice_bitcast_fusion
  13.5 0.7 copy.14.anc_own_gate
  14.2 69.4 %all-gather.2.cloned.1.call-done.full_hbm = bf16[1024,3712]{1,0:T(8,128)(2,1)} async-done(((bf16[64,3712]{1,0:T(8,128)(2,1)}), bf16[1024,3712]{1,0:T(8,128)(2,1)}) %all-gather.2.cloned.1.call-update) | async-done | bytes 7602192 | tf_op jit(solution)/shard_map/all_gather | solution.py:233
  83.5 5.9 %shard_map.120 = (f32[128,1024]{1,0:T(8,128)}, bf16[128,512]{1,0:T(8,128)(2,1)}, bf16[128,512]{1,0:T(8,128)(2,1)}, bf16[128,512]{1,0:T(8,128)(2,1)}, f32[8,1,512]{2,1,0:T(1,128)}) custom-call(bf16[1,1024]{1,0:T(2,128)(2,1)} %bitcast.23, bf16[1,1024]{1,0:T(2,128)(2,1)} %bitcast.25, bf16[1,1024]{1,0:T(2,128)(2,1)} %bitcast.24, ...), custom_call_target="tpu_custom_call" | custom-call | flops 1342177280 | bytes 4849664 | tf_op jit(solution)/shard_map/pallas_call | solution.py:238
  89.5 9.8 %all_to_all.5 = f32[8,1,512]{2,1,0:T(1,128)S(1)} all-to-all(f32[8,1,512]{2,1,0:T(1,128)} %get-tuple-element.14), channel_id=1, replica_groups=mesh['pole'=2,'row'=8,'col'=2] {'row'}, dimensions={0} | all-to-all | bytes 32768 | tf_op jit(solution)/shard_map/all_to_all | solution.py:274
  99.3 0.6 reduce_sum.9
  (2 shorter events, 0.0 us)
Async XLA Ops:
  7.2 76.4 %all-gather.2.cloned.1.call-start = ((), (), s32[]{:S(2)}) async-start(), calls=%async_computation.1 | async-start | bytes 8077312 | tf_op jit(solution)/shard_map/all_gather | solution.py:233
Sparse Core Ops, SparseCore 0:
  10.9 72.6 all-gather.1

commit v16 on v14

--- a/solution.py
+++ b/solution.py
@@ -116,7 +116,7 @@
 def leaf_kernel(
     gate_col, par_col_ref, anc_col_ref, par_own_gate, anc_own_gate, pivots, full_hbm, anc_local, pivinv,
     block_ref, offdiag_ref, par_ref, anc_ref, part_ref,
-    sent_v, anc_v, lower_v, par_v, ancl_v, rows_v, sem,
+    sent_v, anc_v, lower_v, par_v, ancl_v, rows_v, block_v, sem,
 ):
     row, col = lax.axis_index("row"), lax.axis_index("col")
     anc_all, order_all = anc_v.shape[0], lower_v.shape[1]
@@ -173,7 +173,9 @@
         -jnp.dot(lower_cols.T * gate_col, anc_v[...], preferred_element_type=jnp.float32)
     ).astype(jnp.bfloat16)
     block = pivinv[...] - jnp.dot(offdiag_t * gate_col, lower, preferred_element_type=jnp.float32)
-    block_ref[...] = block
+    block_v[...] = block
+    block_copy = pltpu.make_async_copy(block_v, block_ref, sem.at[4])
+    block_copy.start()
     copies[2].wait()
     copies[3].wait()
     par_col, anc_col = par_col_ref[...], anc_col_ref[...]
@@ -196,6 +198,7 @@
     part = jnp.where(row == 0, pivots[...] - part, -part)
     for i in range(part_ref.shape[0]):
         part_ref[i] = part
+    block_copy.wait()
 
 
 def local_whole(
@@ -244,7 +247,7 @@
         in_specs=[vmem] * 6
         + [pl.BlockSpec(memory_space=pl.ANY)]
         + [vmem] * 2,
-        out_specs=(vmem,) * 5,
+        out_specs=(pl.BlockSpec(memory_space=pl.ANY),) + (vmem,) * 4,
         scratch_shapes=[
             pltpu.VMEM((anc_all, sent_width), jnp.bfloat16),
             pltpu.VMEM((anc_all, anc_all), jnp.bfloat16),
@@ -252,7 +255,8 @@
             pltpu.VMEM((order_all, col_width), jnp.bfloat16),
             pltpu.VMEM((anc_all, col_width), jnp.bfloat16),
             pltpu.VMEM((anc_rows, order_all), jnp.bfloat16),
-            pltpu.SemaphoreType.DMA((4,)),
+            pltpu.VMEM((order_rows, order_all), jnp.float32),
+            pltpu.SemaphoreType.DMA((5,)),
         ],
         cost_estimate=pl.CostEstimate(
             flops=flops, transcendentals=0, bytes_accessed=full.size + 8 * anc_rows * order_all

time: 107 us -> 107 us (level)
  no operation moved by 1% of the time
where the time goes in v16:
time: 107 us
  waiting for transfers between devices  69.4 us (65%)
  between operations  14.1 us (13%)
  blocking collectives  9.83 us (9%)
  Pallas kernels  7.98 us (7%)
  local copies, waits for them, and re-layouts  3.61 us (3%)
  other arithmetic  1.92 us (2%)
    all_gather x1, waiting for transfers between devices, local_whole(): full = lax.all_gather(piece, ('row', 'col'), axis=0, tiled=True)  69.4 us
    all_to_all x1, blocking collectives, local_whole(): density = jnp.sum(lax.all_to_all(parts, 'row', 0, 0, tiled=True), axis=0)[0]  9.83 us
    pallas_call x1, Pallas kernels, local_whole(): pl.pallas_call(leaf_kernel, out_shape=(jax.ShapeDtypeStruct((order_rows,...  5.97 us
  transfers between devices with their start and end apart: 1, of which 1 were waited for; matrix products, arithmetic and copies ran while one was open for 5% of the time, Pallas kernels for 0%

profile of v16, /device:TPU:0, one launch (start us, length us, event | category | flops | bytes accessed | tf_op | source)
XLA Modules:
  0.0 106.8 jit_solution(6494412685091384752)
XLA Ops:
  7.2 0.0 all-gather.2.cloned.1.call-start
  7.2 2.0 %shard_map.119 = bf16[64,3712]{1,0:T(8,128)(2,1)} custom-call(bf16[128,1024]{1,0:T(8,128)(2,1)} %anc_local.1, bf16[128,1024]{1,0:T(8,128)(2,1)} %lower_hbm.1, bf16[128,1024]{1,0:T(8,128)(2,1)} %par_hbm.1, bf16[128,1024]{1,0:T(8,128)(2,1)} %ancl_hbm.1), custom_call_target="tpu_custom_call" | custom-call | tf_op jit(solution)/shard_map/pallas_call | solution.py:227
  9.2 0.0 all-gather.2.cloned.1.call-update
  9.2 0.7 convert_element_type.19
  9.9 0.7 convert_element_type.21
  10.6 0.1 broadcast_bitcast_fusion
  10.6 0.6 copy.15
  11.2 0.1 fusion
  11.3 0.1 broadcast_bitcast_fusion.1
  11.4 0.6 copy.17
  12.0 0.6 copy.16
  12.6 0.1 dynamic-slice_bitcast_fusion.1
  12.7 0.7 copy.13.par_own_gate
  13.4 0.1 dynamic-slice_bitcast_fusion
  13.5 0.7 copy.14.anc_own_gate
  14.2 69.4 %all-gather.2.cloned.1.call-done.full_hbm = bf16[1024,3712]{1,0:T(8,128)(2,1)} async-done(((bf16[64,3712]{1,0:T(8,128)(2,1)}), bf16[1024,3712]{1,0:T(8,128)(2,1)}) %all-gather.2.cloned.1.call-update) | async-done | bytes 7602192 | tf_op jit(solution)/shard_map/all_gather | solution.py:233
  83.5 6.0 %shard_map.120 = (f32[128,1024]{1,0:T(8,128)}, bf16[128,512]{1,0:T(8,128)(2,1)}, bf16[128,512]{1,0:T(8,128)(2,1)}, bf16[128,512]{1,0:T(8,128)(2,1)}, f32[8,1,512]{2,1,0:T(1,128)}) custom-call(bf16[1,1024]{1,0:T(2,128)(2,1)} %bitcast.23, bf16[1,1024]{1,0:T(2,128)(2,1)} %bitcast.25, bf16[1,1024]{1,0:T(2,128)(2,1)} %bitcast.24, ...), custom_call_target="tpu_custom_call" | custom-call | flops 1342177280 | bytes 4849664 | tf_op jit(solution)/shard_map/pallas_call | solution.py:238
  89.5 9.8 %all_to_all.5 = f32[8,1,512]{2,1,0:T(1,128)S(1)} all-to-all(f32[8,1,512]{2,1,0:T(1,128)} %get-tuple-element.14), channel_id=1, replica_groups=mesh['pole'=2,'row'=8,'col'=2] {'row'}, dimensions={0} | all-to-all | bytes 32768 | tf_op jit(solution)/shard_map/all_to_all | solution.py:275
  99.4 0.6 reduce_sum.9
  (2 shorter events, 0.0 us)
Async XLA Ops:
  7.2 76.4 %all-gather.2.cloned.1.call-start = ((), (), s32[]{:S(2)}) async-start(), calls=%async_computation.1 | async-start | bytes 8077312 | tf_op jit(solution)/shard_map/all_gather | solution.py:233
Sparse Core Ops, SparseCore 0:
  10.9 72.6 all-gather.1

commit v17 on v14

--- a/solution.py
+++ b/solution.py
@@ -114,14 +114,14 @@
 
 
 def leaf_kernel(
-    gate_col, par_col_ref, anc_col_ref, par_own_gate, anc_own_gate, pivots, full_hbm, anc_local, pivinv,
+    gate_col, par_col_ref, anc_col_ref, par_own_gate, anc_own_gate, pivots, full_hbm, pivinv,
     block_ref, offdiag_ref, par_ref, anc_ref, part_ref,
     sent_v, anc_v, lower_v, par_v, ancl_v, rows_v, sem,
 ):
     row, col = lax.axis_index("row"), lax.axis_index("col")
     anc_all, order_all = anc_v.shape[0], lower_v.shape[1]
     width = par_v.shape[1]
-    order_rows, anc_rows = block_ref.shape[0], anc_local.shape[0]
+    order_rows, anc_rows = block_ref.shape[0], anc_ref.shape[0]
     off_width = offdiag_ref.shape[1]
     sent_width = sent_v.shape[1]
     leaf_at = sent_width + order_all
@@ -141,16 +141,9 @@
     copies[0].start()
     copies[1].start()
     gate_col = gate_col[...]
-    anc_here = anc_local[...]
     copies[0].wait()
     copies[2].start()
     copies[3].start()
-    lower = lower_v[...]
-    rows = (-jnp.dot(anc_here * gate_col, lower, preferred_element_type=jnp.float32)).astype(
-        jnp.bfloat16
-    )
-    rows_v[...] = rows
-    offdiag_ref[...] = rows_v[:, pl.ds(pl.multiple_of(col * off_width, 128), off_width)]
     copies[1].wait()
     blocks = anc_all // anc_rows
     sent = sent_width // anc_rows
@@ -168,6 +161,13 @@
                 anc_v[rows_p, q * anc_rows : (q + 1) * anc_rows] = (
                     part.astype(jnp.float32).T.astype(jnp.bfloat16)
                 )
+    anc_here = anc_v[pl.ds(pl.multiple_of(row * anc_rows, 8), anc_rows), :]
+    lower = lower_v[...]
+    rows = (-jnp.dot(anc_here * gate_col, lower, preferred_element_type=jnp.float32)).astype(
+        jnp.bfloat16
+    )
+    rows_v[...] = rows
+    offdiag_ref[...] = rows_v[:, pl.ds(pl.multiple_of(col * off_width, 128), off_width)]
     lower_cols = lower_v[:, pl.ds(pl.multiple_of(row * order_rows, 128), order_rows)]
     offdiag_t = (
         -jnp.dot(lower_cols.T * gate_col, anc_v[...], preferred_element_type=jnp.float32)
@@ -243,7 +243,7 @@
         ),
         in_specs=[vmem] * 6
         + [pl.BlockSpec(memory_space=pl.ANY)]
-        + [vmem] * 2,
+        + [vmem],
         out_specs=(vmem,) * 5,
         scratch_shapes=[
             pltpu.VMEM((anc_all, sent_width), jnp.bfloat16),
@@ -265,7 +265,6 @@
         lax.dynamic_slice_in_dim(leaf_gate[order_all:], row_index * anc_rows, anc_rows),
         leaf_pivots[None, :],
         full,
-        anc_inverse,
         parent_pivinv,
     )
     density = jnp.sum(lax.all_to_all(parts, "row", 0, 0, tiled=True), axis=0)[0]

time: 107 us -> 107 us (level)
  no operation moved by 1% of the time
where the time goes in v17:
time: 107 us
  waiting for transfers between devices  69.4 us (65%)
  between operations  14.1 us (13%)
  blocking collectives  9.83 us (9%)
  Pallas kernels  7.94 us (7%)
  local copies, waits for them, and re-layouts  3.61 us (3%)
  other arithmetic  1.92 us (2%)
    all_gather x1, waiting for transfers between devices, local_whole(): full = lax.all_gather(piece, ('row', 'col'), axis=0, tiled=True)  69.4 us
    all_to_all x1, blocking collectives, local_whole(): density = jnp.sum(lax.all_to_all(parts, 'row', 0, 0, tiled=True), axis=0)[0]  9.83 us
    pallas_call x1, Pallas kernels, local_whole(): pl.pallas_call(leaf_kernel, out_shape=(jax.ShapeDtypeStruct((order_rows,...  5.94 us
  transfers between devices with their start and end apart: 1, of which 1 were waited for; matrix products, arithmetic and copies ran while one was open for 5% of the time, Pallas kernels for 0%

profile of v17, /device:TPU:0, one launch (start us, length us, event | category | flops | bytes accessed | tf_op | source)
XLA Modules:
  0.0 106.8 jit_solution(14830529024303254260)
XLA Ops:
  7.2 0.0 all-gather.2.cloned.1.call-start
  7.2 2.0 %shard_map.119 = bf16[64,3712]{1,0:T(8,128)(2,1)} custom-call(bf16[128,1024]{1,0:T(8,128)(2,1)} %anc_hbm.1, bf16[128,1024]{1,0:T(8,128)(2,1)} %lower_hbm.1, bf16[128,1024]{1,0:T(8,128)(2,1)} %par_hbm.1, bf16[128,1024]{1,0:T(8,128)(2,1)} %ancl_hbm.1), custom_call_target="tpu_custom_call" | custom-call | tf_op jit(solution)/shard_map/pallas_call | solution.py:224
  9.2 0.0 all-gather.2.cloned.1.call-update
  9.2 0.7 convert_element_type.19
  9.9 0.7 convert_element_type.21
  10.6 0.1 broadcast_bitcast_fusion
  10.6 0.6 copy.15
  11.2 0.1 fusion
  11.3 0.1 broadcast_bitcast_fusion.1
  11.4 0.6 copy.17
  12.0 0.6 copy.16
  12.6 0.1 dynamic-slice_bitcast_fusion.1
  12.7 0.7 copy.13.par_own_gate
  13.4 0.1 dynamic-slice_bitcast_fusion
  13.5 0.7 copy.14.anc_own_gate
  14.2 69.4 %all-gather.2.cloned.1.call-done.full_hbm = bf16[1024,3712]{1,0:T(8,128)(2,1)} async-done(((bf16[64,3712]{1,0:T(8,128)(2,1)}), bf16[1024,3712]{1,0:T(8,128)(2,1)}) %all-gather.2.cloned.1.call-update) | async-done | bytes 7602192 | tf_op jit(solution)/shard_map/all_gather | solution.py:230
  83.5 5.9 %shard_map.120 = (f32[128,1024]{1,0:T(8,128)}, bf16[128,512]{1,0:T(8,128)(2,1)}, bf16[128,512]{1,0:T(8,128)(2,1)}, bf16[128,512]{1,0:T(8,128)(2,1)}, f32[8,1,512]{2,1,0:T(1,128)}) custom-call(bf16[1,1024]{1,0:T(2,128)(2,1)} %bitcast.23, bf16[1,1024]{1,0:T(2,128)(2,1)} %bitcast.25, bf16[1,1024]{1,0:T(2,128)(2,1)} %bitcast.24, ...), custom_call_target="tpu_custom_call" | custom-call | flops 1342177280 | bytes 4849664 | tf_op jit(solution)/shard_map/pallas_call | solution.py:235
  89.5 9.8 %all_to_all.5 = f32[8,1,512]{2,1,0:T(1,128)S(1)} all-to-all(f32[8,1,512]{2,1,0:T(1,128)} %get-tuple-element.14), channel_id=1, replica_groups=mesh['pole'=2,'row'=8,'col'=2] {'row'}, dimensions={0} | all-to-all | bytes 32768 | tf_op jit(solution)/shard_map/all_to_all | solution.py:270
  99.3 0.6 reduce_sum.9
  (2 shorter events, 0.0 us)
Async XLA Ops:
  7.2 76.4 %all-gather.2.cloned.1.call-start = ((), (), s32[]{:S(2)}) async-start(), calls=%async_computation.1 | async-start | bytes 8077312 | tf_op jit(solution)/shard_map/all_gather | solution.py:230
Sparse Core Ops, SparseCore 0:
  10.9 72.6 all-gather.1

commit v18 on v11

--- a/solution.py
+++ b/solution.py
@@ -96,7 +96,7 @@
     )
 
 
-def piece_kernel(anc_hbm, lower_hbm, par_hbm, ancl_hbm, out_ref):
+def piece_kernel(parent_mask, leaf_mask, anc_hbm, lower_hbm, par_hbm, ancl_hbm, out_ref):
     row, col = lax.axis_index("row"), lax.axis_index("col")
     half = out_ref.shape[0]
     blk = anc_hbm.shape[0]
@@ -107,14 +107,21 @@
         start = pl.multiple_of(lax.rem(row + k, blocks) * blk, 128)
         out_ref[:, k * blk : (k + 1) * blk] = anc_hbm[rows, pl.ds(start, blk)]
     at = sent * blk
-    for source in (lower_hbm, par_hbm, ancl_hbm):
+    first_row = row * blk + col * half
+    order_blocks = par_hbm.shape[0] * blocks // BLOCK
+    gates = (
+        parent_mask[first_row // BLOCK],
+        leaf_mask[first_row // BLOCK],
+        leaf_mask[order_blocks + first_row // BLOCK],
+    )
+    for source, gate in zip((lower_hbm, par_hbm, ancl_hbm), gates):
         width = source.shape[1]
-        out_ref[:, at : at + width] = source[rows, :]
+        out_ref[:, at : at + width] = source[rows, :] * gate.astype(jnp.float32).astype(jnp.bfloat16)
         at += width
 
 
 def leaf_kernel(
-    lower_gate, par_gate, anc_gate, pivots, full_hbm, anc_local, pivinv,
+    pivots, full_hbm, anc_local, pivinv,
     block_ref, offdiag_ref, par_ref, anc_ref, part_ref,
     sent_v, anc_v, lower_v, par_v, ancl_v, rows_v, sem,
 ):
@@ -140,14 +147,12 @@
     ]
     copies[0].start()
     copies[1].start()
-    gate_row = lower_gate[...]
-    gate_col = gate_row.T
     anc_here = anc_local[...]
     copies[0].wait()
     copies[2].start()
     copies[3].start()
     lower = lower_v[...]
-    rows = (-jnp.dot(anc_here * gate_col, lower, preferred_element_type=jnp.float32)).astype(
+    rows = (-jnp.dot(anc_here, lower, preferred_element_type=jnp.float32)).astype(
         jnp.bfloat16
     )
     rows_v[...] = rows
@@ -169,23 +174,21 @@
                 anc_v[rows_p, q * anc_rows : (q + 1) * anc_rows] = (
                     part.astype(jnp.float32).T.astype(jnp.bfloat16)
                 )
-    lower_cols = lower_v[:, pl.ds(pl.multiple_of(row * order_rows, 128), order_rows)] * gate_row
+    lower_cols = lower_v[:, pl.ds(pl.multiple_of(row * order_rows, 128), order_rows)]
     offdiag_t = (
         -jnp.dot(lower_cols.T, anc_v[...], preferred_element_type=jnp.float32)
     ).astype(jnp.bfloat16)
-    block = pivinv[...] - jnp.dot(offdiag_t * gate_col, lower, preferred_element_type=jnp.float32)
+    block = pivinv[...] - jnp.dot(offdiag_t, lower, preferred_element_type=jnp.float32)
     block_ref[...] = block
     copies[2].wait()
     copies[3].wait()
-    par_v[...] = par_v[...] * par_gate[...]
-    ancl_v[...] = ancl_v[...] * anc_gate[...]
     par, ancl = par_v[...], ancl_v[...]
     upper = jnp.dot(
         block.astype(jnp.bfloat16), par, preferred_element_type=jnp.float32
     ) + jnp.dot(offdiag_t, ancl, preferred_element_type=jnp.float32)
     par_block = (-upper).astype(jnp.bfloat16)
     lower_sum = jnp.dot(rows, par, preferred_element_type=jnp.float32) + jnp.dot(
-        anc_local[...], ancl, preferred_element_type=jnp.float32
+        anc_here, ancl, preferred_element_type=jnp.float32
     )
     anc_block = (-lower_sum).astype(jnp.bfloat16)
     par_ref[...] = par_block
@@ -226,9 +229,10 @@
     piece = pl.pallas_call(
         piece_kernel,
         out_shape=jax.ShapeDtypeStruct((half, piece_width), jnp.bfloat16),
-        in_specs=[pl.BlockSpec(memory_space=pltpu.VMEM)] * 4,
+        in_specs=[pl.BlockSpec(memory_space=pltpu.SMEM)] * 2
+        + [pl.BlockSpec(memory_space=pltpu.VMEM)] * 4,
         out_specs=pl.BlockSpec(memory_space=pltpu.VMEM),
-    )(anc_inverse, parent_lower, leaf_lower_par, leaf_lower_anc)
+    )(parent_mask, leaf_mask, anc_inverse, parent_lower, leaf_lower_par, leaf_lower_anc)
     full = lax.all_gather(piece, ("row", "col"), axis=0, tiled=True)
     parent_gate = jnp.repeat(parent_mask, BLOCK).astype(jnp.bfloat16)[:, None]
     leaf_gate = jnp.repeat(leaf_mask, BLOCK).astype(jnp.bfloat16)[:, None]
@@ -243,7 +247,7 @@
             jax.ShapeDtypeStruct((anc_rows, col_width), jnp.bfloat16),
             jax.ShapeDtypeStruct((row_devices, 1, col_width), jnp.float32),
         ),
-        in_specs=[vmem] * 4
+        in_specs=[vmem]
         + [pl.BlockSpec(memory_space=pl.ANY)]
         + [vmem] * 2,
         out_specs=(vmem,) * 5,
@@ -260,9 +264,6 @@
             flops=flops, transcendentals=0, bytes_accessed=full.size + 8 * anc_rows * order_all
         ),
     )(
-        parent_gate,
-        leaf_gate[:order_all],
-        leaf_gate[order_all:],
         leaf_pivots[None, :],
         full,
         anc_inverse,
@@ -277,6 +278,7 @@
     return (
         anc_rows == order_rows
         and anc_rows % 128 == 0
+        and BLOCK % (anc_rows // 2) == 0
         and anc_all * anc_all * 2 <= 16 * 1024 * 1024
     )
 

time: 107 us -> 107 us (level)
  waiting for transfers between devices: 70 us -> 74.3 us
  local copies, waits for them, and re-layouts: 2.93 us -> 0 us
  other arithmetic: 1.92 us -> 0.61 us
    all_gather x1, waiting for transfers between devices: 70 us -> 74.2 us  [local_whole(): full = lax.all_gather(piece, ('row', 'col'), axis=0, tiled=True)]
    unnamed x8 -> x0, local copies, waits for them, and re-layouts: 2.85 us -> none
    convert_element_type x2 -> x0, other arithmetic: 1.32 us -> none  [the longest x1 0.66 us: local_whole(): parent_gate = jnp.repeat(parent_mask, BLOCK).astype(jnp.bfloat16)[:, None]]
  transfers between devices with their start and end apart: 1 -> 1, of which waited for: 1 -> 1; matrix products, arithmetic and copies ran while one was open for 4% -> 0% of each run, Pallas kernels for 0% -> 0%
where the time goes in v18:
time: 107 us
  waiting for transfers between devices  74.3 us (69%)
  between operations  14 us (13%)
  blocking collectives  9.8 us (9%)
  Pallas kernels  7.82 us (7%)
    all_gather x1, waiting for transfers between devices, local_whole(): full = lax.all_gather(piece, ('row', 'col'), axis=0, tiled=True)  74.2 us
    all_to_all x1, blocking collectives, local_whole(): density = jnp.sum(lax.all_to_all(parts, 'row', 0, 0, tiled=True), axis=0)[0]  9.8 us
    pallas_call x1, Pallas kernels, local_whole(): pl.pallas_call(leaf_kernel, out_shape=(jax.ShapeDtypeStruct((order_rows,...  5.78 us
  transfers between devices with their start and end apart: 1, of which 1 were waited for; matrix products, arithmetic and copies ran while one was open for 0% of the time, Pallas kernels for 0%

profile of v18, /device:TPU:0, one launch (start us, length us, event | category | flops | bytes accessed | tf_op | source)
XLA Modules:
  0.0 106.6 jit_solution(2351793424456440970)
XLA Ops:
  7.2 0.0 all-gather.2.cloned.1.call-start
  7.2 2.0 %shard_map.119 = bf16[64,3712]{1,0:T(8,128)(2,1)} custom-call(s32[4]{0:T(128)} %parent_mask.1, s32[8]{0:T(128)} %leaf_mask.1, bf16[128,1024]{1,0:T(8,128)(2,1)} %anc_local.1, bf16[128,1024]{1,0:T(8,128)(2,1)} %lower_hbm.1, bf16[128,1024]{1,0:T(8,128)(2,1)} %par_hbm.1, bf16[128,1024]{1,0:T(8,128)(2,1)} %ancl_hbm.1), custom_call_target="tpu_custom_call" | custom-call | tf_op jit(solution)/shard_map/pallas_call | solution.py:229
  9.2 0.0 all-gather.2.cloned.1.call-update
  9.3 74.2 %all-gather.2.cloned.1.call-done.full_hbm = bf16[1024,3712]{1,0:T(8,128)(2,1)} async-done(((bf16[64,3712]{1,0:T(8,128)(2,1)}), bf16[1024,3712]{1,0:T(8,128)(2,1)}) %all-gather.2.cloned.1.call-update) | async-done | bytes 7602192 | tf_op jit(solution)/shard_map/all_gather | solution.py:236
  83.5 5.8 %shard_map.120 = (f32[128,1024]{1,0:T(8,128)}, bf16[128,512]{1,0:T(8,128)(2,1)}, bf16[128,512]{1,0:T(8,128)(2,1)}, bf16[128,512]{1,0:T(8,128)(2,1)}, f32[8,1,512]{2,1,0:T(1,128)}) custom-call(f32[1,512]{1,0:T(1,128)} %bitcast.1, bf16[1024,3712]{1,0:T(8,128)(2,1)} %all-gather.2.cloned.1.call-done.full_hbm, bf16[128,1024]{1,0:T(8,128)(2,1)} %anc_local.1, ...), custom_call_target="tpu_custom_call" | custom-call | flops 1342177280 | bytes 4849664 | tf_op jit(solution)/shard_map/pallas_call | solution.py:241
  89.3 9.8 %all_to_all.5 = f32[8,1,512]{2,1,0:T(1,128)S(1)} all-to-all(f32[8,1,512]{2,1,0:T(1,128)} %get-tuple-element.14), channel_id=1, replica_groups=mesh['pole'=2,'row'=8,'col'=2] {'row'}, dimensions={0} | all-to-all | bytes 32768 | tf_op jit(solution)/shard_map/all_to_all | solution.py:272
  99.1 0.6 reduce_sum.9
Async XLA Ops:
  7.2 76.4 %all-gather.2.cloned.1.call-start = ((), (), s32[]{:S(2)}) async-start(), calls=%async_computation.1 | async-start | bytes 8077312 | tf_op jit(solution)/shard_map/all_gather | solution.py:236
Sparse Core Ops, SparseCore 0:
  10.9 72.6 all-gather.1
